TPU v7x, 512 devices: a whole 4x8x8 slice. The times are simulated.
512 devices in a mesh: pitch: 8 (over z), blk: 64 (over x, y, core).
Axes of the slice: x: 4, y: 8, z: 8, core: 2. Of those that a mesh axis runs over, the one named last changes fastest.
Arguments:
- flux: float32 [128, 64, 45, 128], P('pitch', 'blk'), may hold values from -6 to 6
- pitch_inverse: float32 [64, 128, 128], P('blk', 'pitch')
- span_inverse: float32 [64, 128, 128], P('blk')
- store_old: bfloat16 [8, 64, 128, 45, 128], P('pitch', 'blk'), may hold values from -6 to 6
- send_row: int32 [8, 64, 64], P('pitch', 'blk'), may hold values from 0 to 15
- send_owner: int32 [8, 64, 64], P('pitch', 'blk'), may hold values from 0 to 63, as said below
- send_slot: int32 [8, 64, 64], P('pitch', 'blk'), may hold values from 0 to 127, as said below
- send_count: int32 [8, 64], P('pitch', 'blk'), may hold values from 32 to 64, as said below
Outputs:
- smoothed: float32 [128, 64, 45, 128], P('pitch', 'blk')
- storage: float32 [8, 64, 128, 45, 128], P('pitch', 'blk')
Inputs may be any that keep to these rules, and one draw needn't show every extreme that they name: Live entries are the first send_count of each list; in every draw some device has all 64 entries live. `send_owner`: among one device's live entries no owner is named more than 2 times; in every pitch group one owner is named 2 times by the live entries of every device. `send_slot`: within one pitch group, the live entries that name one owner carry distinct slots. `send_row`: the index is r = p * 1 + b on the sending device, with p its local pitch cell and b its local axial cell.
All inputs are finite; a program needn't handle non-finite values.
Results may differ from a plain program's by a relative error of at most 0.0003.
Values sent between devices are 32-bit elements; how exact they have to be, the bound alone decides.
No kernel may reach another device: no remote copies, remote signals or barrier semaphores. Data moves between devices by JAX's collectives and lax.ppermute only.
A program may use at most 64 MiB of HBM per device.

v0:
```python
import jax
import jax.numpy as jnp
from jax import lax
from jax.sharding import PartitionSpec as P

CAP = 2


def with_halo(block, sides, width):
    for axis, dim in sides:
        count = lax.axis_size(axis)
        forward = [(i, i + 1) for i in range(count - 1)]
        backward = [(target, source) for source, target in forward]
        low = lax.ppermute(
            lax.slice_in_dim(block, block.shape[dim] - width, None, axis=dim), axis, forward
        )
        high = lax.ppermute(lax.slice_in_dim(block, 0, width, axis=dim), axis, backward)
        block = jnp.concatenate([low, block, high], axis=dim)
    return block


def local(
    flux, pitch_inverse, span_inverse, store_old, send_row, send_owner, send_slot, send_count
):
    highest = lax.Precision.HIGHEST
    padded = with_halo(flux, (("blk", 1),), 1)
    residual = 0.25 * padded[:, 2:] - 0.75 * padded[:, :-2] + 0.5 * flux
    pitch_local, axial_local, components, span_cells = flux.shape
    flattened = residual.reshape(pitch_local, axial_local, components * span_cells)
    own_rows = pitch_inverse[0]
    pitch_smoothed = jnp.einsum(
        "pk,kbx->pbx",
        own_rows,
        lax.all_gather(flattened, "pitch", axis=0, tiled=True),
        precision=highest,
    )
    pitch_smoothed = pitch_smoothed.reshape(pitch_local, axial_local, components, span_cells)
    smoothed = jnp.einsum("pbqs,ts->pbqt", pitch_smoothed, span_inverse[0], precision=highest)
    line_rows = smoothed.reshape(pitch_local * axial_local, components, span_cells)
    owners_total = lax.axis_size("blk")
    slot_total = store_old.shape[2]
    entries = send_owner.shape[2]
    owner_ids = send_owner[0, 0]
    is_live = jnp.arange(entries, dtype=jnp.int32) < send_count[0, 0]
    matches = (owner_ids[:, None] == jnp.arange(owners_total, dtype=jnp.int32)[None, :]).astype(
        jnp.int32
    )
    order_rank = jnp.sum(jnp.cumsum(matches, axis=0) * matches, axis=1) - 1
    target = jnp.where(is_live, owner_ids * CAP + order_rank, owners_total * CAP)
    outgoing = jnp.zeros((owners_total * CAP, components, span_cells), jnp.float32)
    outgoing = outgoing.at[target].set(line_rows[send_row[0, 0]], mode="drop")
    slot_tags = (
        jnp.full((owners_total * CAP,), slot_total, jnp.int32)
        .at[target]
        .set(send_slot[0, 0], mode="drop")
    )
    arrived, arrived_tags = (
        lax.all_to_all(
            outgoing.reshape(owners_total, CAP, components, span_cells),
            "blk",
            split_axis=0,
            concat_axis=0,
            tiled=True,
        ),
        lax.all_to_all(
            slot_tags.reshape(owners_total, CAP), "blk", split_axis=0, concat_axis=0, tiled=True
        ),
    )
    storage = (
        store_old[0, 0]
        .astype(jnp.float32)
        .at[arrived_tags.reshape(-1)]
        .set(arrived.reshape(-1, components, span_cells), mode="drop")
    )
    return (smoothed, storage[None, None])


def solution(mesh):
    return jax.shard_map(
        local,
        mesh=mesh,
        in_specs=(
            P("pitch", "blk", None, None),
            P("blk", "pitch", None),
            P("blk", None, None),
            P("pitch", "blk", None, None, None),
            P("pitch", "blk", None),
            P("pitch", "blk", None),
            P("pitch", "blk", None),
            P("pitch", "blk"),
        ),
        out_specs=(P("pitch", "blk", None, None), P("pitch", "blk", None, None, None)),
        check_vma=False,
    )
```

profile of v0, /device:TPU:1, one launch (start us, length us, event | category | flops | bytes accessed | tf_op | source)
XLA Modules:
  0.0 200.1 jit_solution(14577695720133362467)
XLA Ops:
  7.2 8.7 %collective-permute-start = (f32[16,1,45,128]{3,1,2,0:T(1,128)}, f32[16,1,45,128]{3,1,2,0:T(1,128)S(1)}, u32[]{:S(2)}, u32[]{:S(2)}) collective-permute-start(f32[16,1,45,128]{3,1,2,0:T(1,128)} %param.8), channel_id=1, source_target_pairs={{1,0},{2,1},{3,2},{4,3},{5,4},{6,5},{7,6},{8,7},{9,8},{10,9},{11,1... | collective-permute-start | bytes 1105928 | tf_op jit(solution)/shard_map/ppermute | solution.py:17
  16.0 1.9 collective-permute-start.1
  17.9 4.7 %collective-permute-done.1 = f32[16,1,45,128]{3,1,2,0:T(1,128)S(1)} collective-permute-done((f32[16,1,45,128]{3,1,2,0:T(1,128)}, f32[16,1,45,128]{3,1,2,0:T(1,128)S(1)}, u32[]{:S(2)}, u32[]{:S(2)}) %collective-permute-start.1) | collective-permute-done | bytes 368672 | tf_op jit(solution)/shard_map/ppermute | solution.py:14
  22.7 2.4 %add_reduce_fusion = f32[16,45,128]{2,1,0:T(8,128)S(1)} fusion(f32[16,1,45,128]{3,1,2,0:T(1,128)} %param.8, f32[16,1,45,128]{3,1,2,0:T(1,128)S(1)} %collective-permute-done.1, f32[16,1,45,128]{3,1,2,0:T(1,128)S(1)} %collective-permute-done), kind=kLoop, calls=%fused_computation.7 | loop fusion | flops 460800 | bytes 1474560 | tf_op jit(solution)/shard_map/add | solution.py:27
  25.1 0.8 reshape.136
  26.6 0.7 fusion.3
  27.3 0.1 reduce_window_sum.11
  27.4 0.8 select_reduce_fusion
  28.2 0.7 fusion.7
  28.9 0.9 scatter_custom_fusion
  29.8 0.7 all_to_all.9
  30.6 8.4 %all-to-all-start = ((s32[64,1,2]{2,1,0:T(1,128)}), s32[64,1,2]{2,1,0:T(1,128)S(1)}, u32[]{:S(2)}, u32[]{:S(2)}) async-start(s32[64,1,2]{2,1,0:T(1,128)} %bitcast.13), calls=%async_computation | async-start | bytes 65536 | tf_op jit(solution)/shard_map/all_to_all | solution.py:65
  38.9 0.7 fusion.6
  39.6 34.3 %all-gather.2.cloned.1.call-done = f32[128,1,5760]{2,0,1:T(8,128)} async-done(((f32[16,1,5760]{2,0,1:T(8,128)}), f32[128,1,5760]{2,0,1:T(8,128)}) %all-gather.2.cloned.1.call-update) | async-done | bytes 2949136 | tf_op jit(solution)/shard_map/all_gather | solution.py:34
  73.9 3.5 %convolution_bitcast_fusion = f32[16,5760]{1,0:T(8,128)S(1)} fusion(f32[128,1,5760]{2,0,1:T(8,128)} %all-gather.2.cloned.1.call-done, f32[1,16,128]{2,1,0:T(8,128)} %param.9), kind=kOutput, calls=%fused_computation.4 | convolution fusion | flops 141557760 | bytes 3325952 | tf_op jit(solution)/shard_map/pk,kbx->pbx/dot_general | solution.py:31
  77.5 0.5 fusion.1
  77.9 0.7 copy-done.1
  78.7 1.8 gather_fusion
  80.5 0.2 broadcast_in_dim.16
  80.7 6.4 %scatter_fusion = f32[128,45,128]{2,1,0:T(8,128)S(1)} fusion(f32[128,45,128]{2,1,0:T(8,128)S(1)} %broadcast_in_dim.16, s32[64]{0:T(128)S(1)} %fusion.7, f32[64,45,128]{2,1,0:T(8,128)} %gather_fusion), kind=kCustom, calls=%fused_computation.2 | custom fusion | bytes 4423936 | tf_op jit(solution)/shard_map/scatter | solution.py:51
  87.1 3.1 %copy.21 = f32[64,2,45,128]{3,1,2,0:T(2,128)} copy(f32[64,2,45,128]{3,2,1,0:T(8,128)S(1)} %bitcast.44) | data formatting | bytes 5898240 | tf_op jit(solution)/shard_map/reshape | solution.py:59
  90.3 12.0 %all-to-all-start.1 = ((f32[64,2,45,128]{3,1,2,0:T(2,128)}), f32[64,2,45,128]{3,1,2,0:T(2,128)}, u32[]{:S(2)}, u32[]{:S(2)}) async-start(f32[64,2,45,128]{3,1,2,0:T(2,128)} %copy.21), calls=%async_computation.1 | async-start | bytes 5898240 | tf_op jit(solution)/shard_map/all_to_all | solution.py:58
  102.3 2.2 %bitcast_convert_fusion = f32[128,45,128]{2,1,0:T(8,128)S(1)} fusion(bf16[1,1,128,45,128]{4,2,3,1,0:T(8,128)(2,1)} %param.11), kind=kLoop, calls=%fused_computation.6 | loop fusion | flops 737280 | bytes 4423680 | tf_op jit(solution)/shard_map/convert_element_type | solution.py:71
  104.5 0.5 broadcast.109
  105.0 0.7 reduce.5
  105.8 0.1 reshape.139
  105.9 2.1 %copy.24 = f32[16,1,45,128]{3,1,2,0:T(1,128)} copy(f32[16,1,45,128]{3,2,0,1:T(8,128)} %bitcast.45) | data formatting | bytes 737280
  108.0 63.4 %all-to-all-done.1 = f32[64,2,45,128]{3,1,2,0:T(2,128)} async-done(((f32[64,2,45,128]{3,1,2,0:T(2,128)}), f32[64,2,45,128]{3,1,2,0:T(2,128)}, u32[]{:S(2)}, u32[]{:S(2)}) %all-to-all-start.1) | async-done | bytes 2949152 | tf_op jit(solution)/shard_map/all_to_all | solution.py:58
  171.5 3.5 %copy.22 = f32[64,2,45,128]{3,1,0,2:T(2,128)S(1)} copy(f32[64,2,45,128]{3,1,2,0:T(2,128)} %all-to-all-done.1) | data formatting | bytes 5898240 | tf_op jit(solution)/shard_map/all_to_all | solution.py:58
  174.9 3.4 %copy.23 = f32[128,45,128]{2,1,0:T(8,128)} copy(f32[128,45,128]{2,0,1:T(8,128)S(1)} %bitcast.46) | data formatting | bytes 5898240 | tf_op jit(solution)/shard_map/reshape | solution.py:73
  178.3 12.4 %scatter_fusion.1 = f32[128,45,128]{2,1,0:T(8,128)S(1)} fusion(f32[128,45,128]{2,1,0:T(8,128)S(1)} %bitcast_convert_fusion, s32[128]{0:T(128)S(1)} %fusion.5, f32[128,45,128]{2,1,0:T(8,128)} %copy.23), kind=kCustom, calls=%fused_computation.3 | custom fusion | bytes 8847872 | tf_op jit(solution)/shard_map/scatter | solution.py:73
  190.8 2.5 %copy.25 = f32[1,1,128,45,128]{4,2,3,1,0:T(8,128)} copy(f32[1,1,128,45,128]{4,3,2,1,0:T(8,128)S(1)} %bitcast.43) | data formatting | bytes 5898240
  (10 shorter events, 0.1 us)
Async XLA Ops:
  7.2 70.3 %copy-start = (f32[1,128,128]{2,1,0:T(8,128)S(1)}, f32[1,128,128]{2,1,0:T(8,128)}, u32[]{:S(2)}) copy-start(f32[1,128,128]{2,1,0:T(8,128)} %param.10) | copy-start | bytes 196612
  7.2 66.7 %all-gather.2.cloned.1.call-start = ((), (), s32[]{:S(2)}) async-start(), calls=%async_computation.2 | async-start | bytes 3317760 | tf_op jit(solution)/shard_map/all_gather | solution.py:34
  7.2 10.7 %collective-permute-start = (f32[16,1,45,128]{3,1,2,0:T(1,128)}, f32[16,1,45,128]{3,1,2,0:T(1,128)S(1)}, u32[]{:S(2)}, u32[]{:S(2)}) collective-permute-start(f32[16,1,45,128]{3,1,2,0:T(1,128)} %param.8), channel_id=1, source_target_pairs={{1,0},{2,1},{3,2},{4,3},{5,4},{6,5},{7,6},{8,7},{9,8},{10,9},{11,1... | collective-permute-start | bytes 1105928 | tf_op jit(solution)/shard_map/ppermute | solution.py:17
  16.0 6.7 %collective-permute-start.1 = (f32[16,1,45,128]{3,1,2,0:T(1,128)}, f32[16,1,45,128]{3,1,2,0:T(1,128)S(1)}, u32[]{:S(2)}, u32[]{:S(2)}) collective-permute-start(f32[16,1,45,128]{3,1,2,0:T(1,128)} %param.8), channel_id=1, source_target_pairs={{0,1},{1,2},{2,3},{3,4},{4,5},{5,6},{6,7},{7,8},{8,9},{9,10},{10,1... | collective-permute-start | bytes 1105928 | tf_op jit(solution)/shard_map/ppermute | solution.py:14
  30.6 59.7 %all-to-all-start = ((s32[64,1,2]{2,1,0:T(1,128)}), s32[64,1,2]{2,1,0:T(1,128)S(1)}, u32[]{:S(2)}, u32[]{:S(2)}) async-start(s32[64,1,2]{2,1,0:T(1,128)} %bitcast.13), calls=%async_computation | async-start | bytes 65536 | tf_op jit(solution)/shard_map/all_to_all | solution.py:65
  77.9 0.8 copy-start.1
  90.3 81.2 %all-to-all-start.1 = ((f32[64,2,45,128]{3,1,2,0:T(2,128)}), f32[64,2,45,128]{3,1,2,0:T(2,128)}, u32[]{:S(2)}, u32[]{:S(2)}) async-start(f32[64,2,45,128]{3,1,2,0:T(2,128)} %copy.21), calls=%async_computation.1 | async-start | bytes 5898240 | tf_op jit(solution)/shard_map/all_to_all | solution.py:58
Sparse Core Ops, SparseCore 0:
  26.0 47.8 all-gather.1
where the time goes:
time: 201 us; the launch traced here: 200 us
  waiting for transfers between devices  103 us (51%)
  local copies, waits for them, and re-layouts  39.4 us (20%)
  starting transfers between devices  31.1 us (15%)
  between operations  14.8 us (7%)
  other arithmetic  8.4 us (4%)
  matrix products  3.95 us (2%)
    all_to_all x1, waiting for transfers between devices, local(): lax.all_to_all(outgoing.reshape(owners_total, CAP, components, span_cells...  63.4 us
    all_gather x1, waiting for transfers between devices, local(): lax.all_gather(flattened, 'pitch', axis=0, tiled=True)  34.3 us
    scatter x1, local copies, waits for them, and re-layouts, local(): storage = store_old[0, 0].astype(jnp.float32).at[arrived_tags.reshape(-1)...  12.4 us
    all_to_all x1, starting transfers between devices, local(): lax.all_to_all(outgoing.reshape(owners_total, CAP, components, span_cells...  12 us
    ppermute x1, starting transfers between devices, with_halo(): lax.ppermute(lax.slice_in_dim(block, 0, width, axis=dim), axis, backward)  8.75 us
    all_to_all x1, starting transfers between devices, local(): lax.all_to_all(slot_tags.reshape(owners_total, CAP), 'blk', split_axis=0,...  8.36 us
    scatter x1, local copies, waits for them, and re-layouts, local(): outgoing = outgoing.at[target].set(line_rows[send_row[0, 0]], mode='drop')  6.43 us
    unnamed x6, local copies, waits for them, and re-layouts  5.38 us
  transfers between devices with their start and end apart: 5, of which 3 were waited for; matrix products, arithmetic and copies ran while one was open for 13% of the time, Pallas kernels for 0%

commit v1 on v0

v1 whole, which is shorter than its diff:
```python
import jax
import jax.numpy as jnp
from jax import lax
from jax.sharding import PartitionSpec as P

CAP = 2


def with_halo(block, axis, dim):
    count = lax.axis_size(axis)
    forward = [(i, i + 1) for i in range(count - 1)]
    backward = [(target, source) for source, target in forward]
    low = lax.ppermute(block, axis, forward)
    high = lax.ppermute(block, axis, backward)
    return low, high


def entry_ranks(owner):
    entries = owner.shape[-1]
    same = owner[..., :, None] == owner[..., None, :]
    earlier = jnp.arange(entries)[None, :] < jnp.arange(entries)[:, None]
    return jnp.sum(same & earlier, axis=-1).astype(jnp.int32)


def local(
    flux, pitch_inverse, span_inverse, store_old, send_row, send_owner, send_slot, send_count
):
    highest = lax.Precision.HIGHEST
    n_pitch = lax.axis_size("pitch")
    n_blk = lax.axis_size("blk")
    me = lax.axis_index("blk")
    pitch_local, axial_local, components, span_cells = flux.shape
    entries = send_owner.shape[2]
    slot_total = store_old.shape[2]

    plan = jnp.concatenate([send_owner[0, 0], send_slot[0, 0], send_count[0]], axis=0)
    plans = lax.all_gather(plan, "blk", axis=0, tiled=False)
    pinv_full = lax.all_gather(pitch_inverse[0], "pitch", axis=0, tiled=True)

    low, high = with_halo(flux, "blk", 1)
    residual = 0.25 * high - 0.75 * low + 0.5 * flux
    padded_q = -(-components // n_pitch) * n_pitch
    chunk_q = padded_q // n_pitch
    res = residual.reshape(pitch_local, components, span_cells)
    res = jnp.pad(res, ((0, 0), (0, padded_q - components), (0, 0)))
    spanned = jnp.einsum("pqs,ts->pqt", res, span_inverse[0], precision=highest)
    chunks = spanned.reshape(pitch_local, n_pitch, chunk_q * span_cells).transpose(1, 0, 2)
    gathered = lax.all_to_all(chunks, "pitch", 0, 0, tiled=True)
    gathered = gathered.reshape(n_pitch * pitch_local, chunk_q * span_cells)
    mixed = jnp.dot(pinv_full, gathered, precision=highest)
    back = lax.all_to_all(
        mixed.reshape(n_pitch, pitch_local, chunk_q * span_cells), "pitch", 0, 0, tiled=True
    )
    smoothed = (
        back.reshape(n_pitch, pitch_local, chunk_q, span_cells)
        .transpose(1, 0, 2, 3)
        .reshape(pitch_local, padded_q, span_cells)[:, :components]
    )

    rows = smoothed.reshape(pitch_local * axial_local, components * span_cells)
    my_owner = send_owner[0, 0]
    live = jnp.arange(entries, dtype=jnp.int32) < send_count[0, 0]
    target = jnp.where(live, my_owner * CAP + entry_ranks(my_owner), -1)
    slot_ids = jnp.arange(n_blk * CAP, dtype=jnp.int32)
    row_ids = jnp.arange(pitch_local * axial_local, dtype=jnp.int32)
    select_out = jnp.any(
        (target[None, :, None] == slot_ids[:, None, None])
        & (send_row[0, 0][None, :, None] == row_ids[None, None, :]),
        axis=1,
    ).astype(jnp.float32)
    outgoing = jnp.dot(select_out, rows, precision=highest)
    arrived = lax.all_to_all(
        outgoing.reshape(n_blk * CAP, components, span_cells), "blk", 0, 0, tiled=True
    )

    owners_all = plans[:, :entries]
    slots_all = plans[:, entries : 2 * entries]
    counts_all = plans[:, 2 * entries]
    ranks_all = entry_ranks(owners_all)
    hit = (jnp.arange(entries, dtype=jnp.int32)[None, :] < counts_all[:, None]) & (
        owners_all == me
    )
    slot_of = jnp.stack(
        [jnp.sum(jnp.where(hit & (ranks_all == c), slots_all + 1, 0), axis=1) - 1 for c in range(CAP)],
        axis=1,
    ).reshape(n_blk * CAP)
    select_in = slot_of[None, :] == jnp.arange(slot_total, dtype=jnp.int32)[:, None]
    filled = jnp.any(select_in, axis=1)
    incoming = jnp.dot(
        select_in.astype(jnp.float32),
        arrived.reshape(n_blk * CAP, components * span_cells),
        precision=highest,
    ).reshape(slot_total, components, span_cells)
    storage = jnp.where(filled[:, None, None], incoming, store_old[0, 0].astype(jnp.float32))
    return (smoothed.reshape(flux.shape), storage[None, None])


def solution(mesh):
    return jax.shard_map(
        local,
        mesh=mesh,
        in_specs=(
            P("pitch", "blk", None, None),
            P("blk", "pitch", None),
            P("blk", None, None),
            P("pitch", "blk", None, None, None),
            P("pitch", "blk", None),
            P("pitch", "blk", None),
            P("pitch", "blk", None),
            P("pitch", "blk"),
        ),
        out_specs=(P("pitch", "blk", None, None), P("pitch", "blk", None, None, None)),
        check_vma=False,
    )
```

time: 201 us -> 413 us (2.05)
  blocking collectives: 0 us -> 324 us
  waiting for transfers between devices: 103 us -> 16.4 us
  local copies, waits for them, and re-layouts: 39.4 us -> 12.5 us
  between operations: 14.8 us -> 2.07 us
  starting transfers between devices: 31.1 us -> 42.9 us
  matrix products: 3.95 us -> 8.73 us
  other arithmetic: 8.4 us -> 3.97 us
    unnamed x0 -> x1, blocking collectives: none -> 303 us
    all_to_all x2 -> x3, waiting for transfers between devices: 63.4 us -> 12.8 us  [the longest x1 12.8 us: local(): lax.all_to_all(mixed.reshape(n_pitch, pitch_local, chunk_q * span_cells),...]
    all_gather x1 -> x0, waiting for transfers between devices: 34.3 us -> none  [local(): lax.all_gather(flattened, 'pitch', axis=0, tiled=True)]
    all_gather x0 -> x1, blocking collectives: none -> 21.4 us  [local(): pinv_full = lax.all_gather(pitch_inverse[0], 'pitch', axis=0, tiled=True)]
    scatter x3 -> x0, local copies, waits for them, and re-layouts: 19.8 us -> none  [the longest x1 12.4 us: local(): storage = store_old[0, 0].astype(jnp.float32).at[arrived_tags.reshape(-1)...]
    all_to_all x2 -> x3, starting transfers between devices: 20.4 us -> 32.8 us  [the longest x1 18.3 us: local(): lax.all_to_all(outgoing.reshape(n_blk * CAP, components, span_cells), 'bl...]
    reshape x4 -> x3, local copies, waits for them, and re-layouts: 7.44 us -> 1.01 us  [the longest x2 0.95 us: local(): spanned.reshape(pitch_local, n_pitch, chunk_q * span_cells)]
    dot_general x2 -> x4, matrix products: 3.95 us -> 8.73 us  [the longest x1 5.65 us: local(): jnp.dot(select_in.astype(jnp.float32), arrived.reshape(n_blk * CAP, compo...]
  transfers between devices with their start and end apart: 5 -> 5, of which waited for: 3 -> 2; matrix products, arithmetic and copies ran while one was open for 13% -> 2% of each run, Pallas kernels for 0% -> 0%
where the time goes in v1:
time: 413 us; the launch traced here: 411 us
  blocking collectives  324 us (78%)
  starting transfers between devices  42.9 us (10%)
  waiting for transfers between devices  16.4 us (4%)
  local copies, waits for them, and re-layouts  12.5 us (3%)
  matrix products  8.73 us (2%)
    unnamed x1, blocking collectives  303 us
    all_gather x1, blocking collectives, local(): pinv_full = lax.all_gather(pitch_inverse[0], 'pitch', axis=0, tiled=True)  21.4 us
    all_to_all x1, starting transfers between devices, local(): lax.all_to_all(outgoing.reshape(n_blk * CAP, components, span_cells), 'bl...  18.3 us
    all_to_all x1, waiting for transfers between devices, local(): lax.all_to_all(mixed.reshape(n_pitch, pitch_local, chunk_q * span_cells),...  12.8 us
    all_to_all x1, starting transfers between devices, local(): gathered = lax.all_to_all(chunks, 'pitch', 0, 0, tiled=True)  10 us
  transfers between devices with their start and end apart: 5, of which 2 were waited for; matrix products, arithmetic and copies ran while one was open for 2% of the time, Pallas kernels for 0%

profile of v1, /device:TPU:1, one launch (start us, length us, event | category | flops | bytes accessed | tf_op | source)
XLA Modules:
  0.0 410.5 jit_solution(2055467784681924422)
XLA Ops:
  0.7 1.0 copy.48
  1.7 4.6 %collective-permute-start.1 = (f32[16,1,45,128]{3,2,0,1:T(8,128)S(1)}, f32[16,1,45,128]{3,2,0,1:T(8,128)S(1)}, u32[]{:S(2)}, u32[]{:S(2)}) collective-permute-start(f32[16,1,45,128]{3,2,0,1:T(8,128)S(1)} %copy.48), channel_id=1, source_target_pairs={{0,1},{1,2},{2,3},{3,4},{4,5},{5,6},{6,7},{7,8},{8,9},{9,10},{10,1... | collective-permute-start | bytes 1105928 | tf_op jit(solution)/shard_map/ppermute | solution.py:13
  6.3 5.5 %collective-permute-start = (f32[16,1,45,128]{3,2,0,1:T(8,128)S(1)}, f32[16,1,45,128]{3,2,0,1:T(8,128)S(1)}, u32[]{:S(2)}, u32[]{:S(2)}) collective-permute-start(f32[16,1,45,128]{3,2,0,1:T(8,128)S(1)} %copy.48), channel_id=1, source_target_pairs={{1,0},{2,1},{3,2},{4,3},{5,4},{6,5},{7,6},{8,7},{9,8},{10,9},{11,1... | collective-permute-start | bytes 1105928 | tf_op jit(solution)/shard_map/ppermute | solution.py:14
  11.8 3.6 collective-permute-done
  15.4 1.1 add_bitcast_fusion
  16.5 0.5 fusion.5
  17.0 0.1 reshape.135
  17.1 0.9 copy.70
  17.9 10.0 %all-to-all-start = ((f32[8,16,768]{2,1,0:T(8,128)}), f32[8,16,768]{2,1,0:T(8,128)S(1)}, u32[]{:S(2)}, u32[]{:S(2)}) async-start(f32[8,16,768]{2,1,0:T(8,128)} %bitcast.65), calls=%async_computation | async-start | bytes 786432 | tf_op jit(solution)/shard_map/all_to_all | solution.py:48
  28.6 21.4 %all-gather = f32[1,128,128]{2,1,0:T(8,128)S(1)} all-gather(f32[1,16,128]{2,1,0:T(8,128)S(1)} %copy-done.1), channel_id=2, replica_groups=mesh['pitch'=8,'blk'=64] {'pitch'}, dimensions={1}, use_global_device_ids=true | all-gather | bytes 73728 | tf_op jit(solution)/shard_map/all_gather | solution.py:38
  50.0 0.2 convert_reduce_fusion.1
  50.2 1.2 fusion.10
  51.4 4.5 %all-to-all-start.1 = ((f32[8,16,768]{2,1,0:T(8,128)}), f32[8,16,768]{2,1,0:T(8,128)S(1)}, u32[]{:S(2)}, u32[]{:S(2)}) async-start(f32[8,16,768]{2,1,0:T(8,128)} %bitcast.7), calls=%async_computation.1 | async-start | bytes 786432 | tf_op jit(solution)/shard_map/all_to_all | solution.py:51
  56.1 0.2 and_reduce_fusion
  56.3 12.8 %all-to-all-done.1 = f32[8,16,768]{2,1,0:T(8,128)S(1)} async-done(((f32[8,16,768]{2,1,0:T(8,128)}), f32[8,16,768]{2,1,0:T(8,128)S(1)}, u32[]{:S(2)}, u32[]{:S(2)}) %all-to-all-start.1) | async-done | bytes 393248 | tf_op jit(solution)/shard_map/all_to_all | solution.py:51
  69.2 0.8 slice_bitcast_fusion
  70.0 1.4 fusion.7
  71.4 3.4 copy.56
  74.8 18.3 %all-to-all-start.2 = ((f32[128,45,128]{2,1,0:T(8,128)}), f32[128,45,128]{2,1,0:T(8,128)S(1)}, u32[]{:S(2)}, u32[]{:S(2)}) async-start(f32[128,45,128]{2,1,0:T(8,128)} %copy.56), calls=%async_computation.2 | async-start | bytes 6291456 | tf_op jit(solution)/shard_map/all_to_all | solution.py:72
  93.1 1.2 dynamic-slice
  94.9 0.2 add_dynamic-update-slice_fusion
  95.1 302.6 %all-reduce.1 = s32[8256]{0:T(1024)S(1)} all-reduce(s32[8256]{0:T(1024)S(1)} %add_dynamic-update-slice_fusion), channel_id=3, replica_groups=mesh['pitch'=8,'blk'=64] {'blk'}, use_global_device_ids=true, to_apply=%add.1 | all-reduce | flops 8256 | bytes 66048
  397.7 0.2 reshape.145
  397.9 0.1 slice_reduce_fusion
  398.0 1.9 convert_reduce_fusion
  399.9 0.2 select_reduce_fusion.1
  400.1 0.1 copy.53
  400.2 0.1 eq.102
  400.3 0.1 fusion.14
  400.5 2.1 copy.58
  402.6 2.3 copy.57
  404.9 5.7 %fusion = f32[1,1,128,45,128]{4,2,3,1,0:T(8,128)} fusion(f32[128,45,128]{0,2,1:T(8,128)} %copy.57, bf16[1,1,128,45,128]{4,2,3,1,0:T(8,128)(2,1)} %param.11, pred[128]{0:T(512)(128)(4,1)S(1)} %fusion.14, s32[128]{0:T(128)S(1)} %eq.102), kind=kOutput, calls=%fused_computation.1 | convolution fusion | flops 1133953024 | bytes 7373440 | tf_op jit(solution)/shard_map/dot_general | solution.py:89
  (23 shorter events, 0.4 us)
Async XLA Ops:
  0.6 15.8 %copy-start = (f32[1,128,128]{2,1,0:T(8,128)S(1)}, f32[1,128,128]{2,1,0:T(8,128)}, u32[]{:S(2)}) copy-start(f32[1,128,128]{2,1,0:T(8,128)} %param.10) | copy-start | bytes 196612
  0.6 28.0 %copy-start.1 = (f32[1,16,128]{2,1,0:T(8,128)S(1)}, f32[1,16,128]{2,1,0:T(8,128)}, u32[]{:S(2)}) copy-start(f32[1,16,128]{2,1,0:T(8,128)} %param.9) | copy-start | bytes 24580
  0.7 49.3 %copy-start.2 = (s32[1,1,64]{2,1,0:T(1,128)S(1)}, s32[1,1,64]{2,1,0:T(1,128)}, u32[]{:S(2)}) copy-start(s32[1,1,64]{2,1,0:T(1,128)} %param.13) | copy-start | bytes 772
  1.7 54.2 %copy-start.3 = (s32[1,1,64]{2,1,0:T(1,128)S(1)}, s32[1,1,64]{2,1,0:T(1,128)}, u32[]{:S(2)}) copy-start(s32[1,1,64]{2,1,0:T(1,128)} %param.12) | copy-start | bytes 772
  1.7 10.1 %collective-permute-start.1 = (f32[16,1,45,128]{3,2,0,1:T(8,128)S(1)}, f32[16,1,45,128]{3,2,0,1:T(8,128)S(1)}, u32[]{:S(2)}, u32[]{:S(2)}) collective-permute-start(f32[16,1,45,128]{3,2,0,1:T(8,128)S(1)} %copy.48), channel_id=1, source_target_pairs={{0,1},{1,2},{2,3},{3,4},{4,5},{5,6},{6,7},{7,8},{8,9},{9,10},{10,1... | collective-permute-start | bytes 1105928 | tf_op jit(solution)/shard_map/ppermute | solution.py:13
  6.3 9.1 %collective-permute-start = (f32[16,1,45,128]{3,2,0,1:T(8,128)S(1)}, f32[16,1,45,128]{3,2,0,1:T(8,128)S(1)}, u32[]{:S(2)}, u32[]{:S(2)}) collective-permute-start(f32[16,1,45,128]{3,2,0,1:T(8,128)S(1)} %copy.48), channel_id=1, source_target_pairs={{1,0},{2,1},{3,2},{4,3},{5,4},{6,5},{7,6},{8,7},{9,8},{10,9},{11,1... | collective-permute-start | bytes 1105928 | tf_op jit(solution)/shard_map/ppermute | solution.py:14
  17.9 32.2 %all-to-all-start = ((f32[8,16,768]{2,1,0:T(8,128)}), f32[8,16,768]{2,1,0:T(8,128)S(1)}, u32[]{:S(2)}, u32[]{:S(2)}) async-start(f32[8,16,768]{2,1,0:T(8,128)} %bitcast.65), calls=%async_computation | async-start | bytes 786432 | tf_op jit(solution)/shard_map/all_to_all | solution.py:48
  51.4 17.7 %all-to-all-start.1 = ((f32[8,16,768]{2,1,0:T(8,128)}), f32[8,16,768]{2,1,0:T(8,128)S(1)}, u32[]{:S(2)}, u32[]{:S(2)}) async-start(f32[8,16,768]{2,1,0:T(8,128)} %bitcast.7), calls=%async_computation.1 | async-start | bytes 786432 | tf_op jit(solution)/shard_map/all_to_all | solution.py:51
  74.8 20.1 %copy-start.4 = (s32[1,1,64]{2,1,0:T(1,128)S(1)}, s32[1,1,64]{2,1,0:T(1,128)}, u32[]{:S(2)}) copy-start(s32[1,1,64]{2,1,0:T(1,128)} %param.14) | copy-start | bytes 772
  74.8 327.8 %all-to-all-start.2 = ((f32[128,45,128]{2,1,0:T(8,128)}), f32[128,45,128]{2,1,0:T(8,128)S(1)}, u32[]{:S(2)}, u32[]{:S(2)}) async-start(f32[128,45,128]{2,1,0:T(8,128)} %copy.56), calls=%async_computation.2 | async-start | bytes 6291456 | tf_op jit(solution)/shard_map/all_to_all | solution.py:72

commit v2 on v1

v2 whole, which is shorter than its diff:
```python
import jax
import jax.numpy as jnp
from jax import lax
from jax.sharding import PartitionSpec as P

CAP = 2


def with_halo(block, axis, dim):
    count = lax.axis_size(axis)
    forward = [(i, i + 1) for i in range(count - 1)]
    backward = [(target, source) for source, target in forward]
    low = lax.ppermute(block, axis, forward)
    high = lax.ppermute(block, axis, backward)
    return low, high


def entry_ranks(owner):
    entries = owner.shape[-1]
    same = owner[..., :, None] == owner[..., None, :]
    earlier = jnp.arange(entries)[None, :] < jnp.arange(entries)[:, None]
    return jnp.sum(same & earlier, axis=-1).astype(jnp.int32)


def local(
    flux, pitch_inverse, span_inverse, store_old, send_row, send_owner, send_slot, send_count
):
    highest = lax.Precision.HIGHEST
    n_pitch = lax.axis_size("pitch")
    n_blk = lax.axis_size("blk")
    pitch_local, axial_local, components, span_cells = flux.shape
    entries = send_owner.shape[2]
    slot_total = store_old.shape[2]

    low, high = with_halo(flux, "blk", 1)
    residual = 0.25 * high - 0.75 * low + 0.5 * flux
    padded_q = -(-components // n_pitch) * n_pitch
    chunk_q = padded_q // n_pitch
    width = chunk_q * span_cells
    res = residual.reshape(pitch_local, components, span_cells)
    res = jnp.pad(res, ((0, 0), (0, padded_q - components), (0, 0)))
    spanned = jnp.einsum("pqs,ts->pqt", res, span_inverse[0], precision=highest)
    chunks = spanned.reshape(pitch_local, n_pitch, width).transpose(1, 0, 2)
    pinv_rows = jnp.broadcast_to(pitch_inverse[0][None], (n_pitch,) + pitch_inverse.shape[1:])
    chunks = jnp.concatenate([chunks, pinv_rows], axis=2)
    gathered = lax.all_to_all(chunks, "pitch", 0, 0, tiled=True)
    gathered = gathered.reshape(n_pitch * pitch_local, width + pitch_inverse.shape[2])
    pinv_full = gathered[:, width:]
    mixed = jnp.dot(pinv_full, gathered[:, :width], precision=highest)
    back = lax.all_to_all(mixed.reshape(n_pitch, pitch_local, width), "pitch", 0, 0, tiled=True)
    smoothed = (
        back.reshape(n_pitch, pitch_local, chunk_q, span_cells)
        .transpose(1, 0, 2, 3)
        .reshape(pitch_local, padded_q, span_cells)[:, :components]
    )

    rows = smoothed.reshape(pitch_local * axial_local, components * span_cells)
    my_owner = send_owner[0, 0]
    live = jnp.arange(entries, dtype=jnp.int32) < send_count[0, 0]
    target = jnp.where(live, my_owner * CAP + entry_ranks(my_owner), -1)
    slot_ids = jnp.arange(n_blk * CAP, dtype=jnp.int32)
    row_ids = jnp.arange(pitch_local * axial_local, dtype=jnp.int32)
    hits = target[None, :] == slot_ids[:, None]
    select_out = jnp.any(
        hits[:, :, None] & (send_row[0, 0][None, :, None] == row_ids[None, None, :]), axis=1
    ).astype(jnp.float32)
    tag = jnp.sum(jnp.where(hits, send_slot[0, 0][None, :] + 1, 0), axis=1) - 1
    outgoing = jnp.dot(select_out, rows, precision=highest).reshape(
        n_blk * CAP, components, span_cells
    )
    tag_row = jnp.broadcast_to(tag.astype(jnp.float32)[:, None, None], (n_blk * CAP, 1, span_cells))
    outgoing = jnp.concatenate([outgoing, tag_row], axis=1)
    arrived = lax.all_to_all(outgoing, "blk", 0, 0, tiled=True)

    arrived_slot = arrived[:, components, 0].astype(jnp.int32)
    select_in = arrived_slot[None, :] == jnp.arange(slot_total, dtype=jnp.int32)[:, None]
    filled = jnp.any(select_in, axis=1)
    incoming = jnp.dot(
        select_in.astype(jnp.float32),
        arrived[:, :components].reshape(n_blk * CAP, components * span_cells),
        precision=highest,
    ).reshape(slot_total, components, span_cells)
    storage = jnp.where(filled[:, None, None], incoming, store_old[0, 0].astype(jnp.float32))
    return (smoothed.reshape(flux.shape), storage[None, None])


def solution(mesh):
    return jax.shard_map(
        local,
        mesh=mesh,
        in_specs=(
            P("pitch", "blk", None, None),
            P("blk", "pitch", None),
            P("blk", None, None),
            P("pitch", "blk", None, None, None),
            P("pitch", "blk", None),
            P("pitch", "blk", None),
            P("pitch", "blk", None),
            P("pitch", "blk"),
        ),
        out_specs=(P("pitch", "blk", None, None), P("pitch", "blk", None, None, None)),
        check_vma=False,
    )
```

time: 413 us -> 164 us (0.40)
  blocking collectives: 324 us -> 0 us
  waiting for transfers between devices: 16.4 us -> 96.8 us
    unnamed x1 -> x0, blocking collectives: 303 us -> none
    all_to_all x2, waiting for transfers between devices: 12.8 us -> 82.5 us  [the longest x1 71.4 us: local(): arrived = lax.all_to_all(outgoing, 'blk', 0, 0, tiled=True)]
    all_gather x1 -> x0, blocking collectives: 21.4 us -> none  [local(): pinv_full = lax.all_gather(pitch_inverse[0], 'pitch', axis=0, tiled=True)]
    all_to_all x1, waiting for transfers between devices: 0.01 us -> 10.7 us  [local(): gathered = lax.all_to_all(chunks, 'pitch', 0, 0, tiled=True)]
  transfers between devices with their start and end apart: 5 -> 5, of which waited for: 2 -> 4; matrix products, arithmetic and copies ran while one was open for 2% -> 2% of each run, Pallas kernels for 0% -> 0%
where the time goes in v2:
time: 164 us; the launch traced here: 163 us
  waiting for transfers between devices  96.8 us (59%)
  starting transfers between devices  41.1 us (25%)
  local copies, waits for them, and re-layouts  10.1 us (6%)
  matrix products  8.71 us (5%)
  other arithmetic  5.34 us (3%)
    all_to_all x1, waiting for transfers between devices, local(): arrived = lax.all_to_all(outgoing, 'blk', 0, 0, tiled=True)  71.4 us
    all_to_all x1, starting transfers between devices, local(): arrived = lax.all_to_all(outgoing, 'blk', 0, 0, tiled=True)  17.5 us
    all_to_all x1, waiting for transfers between devices, local(): lax.all_to_all(mixed.reshape(n_pitch, pitch_local, width), 'pitch', 0, 0,...  11.1 us
    all_to_all x1, waiting for transfers between devices, local(): gathered = lax.all_to_all(chunks, 'pitch', 0, 0, tiled=True)  10.7 us
    all_to_all x1, starting transfers between devices, local(): gathered = lax.all_to_all(chunks, 'pitch', 0, 0, tiled=True)  10 us
    unnamed x14, local copies, waits for them, and re-layouts  6.27 us
    dot_general x1, matrix products, local(): jnp.dot(select_in.astype(jnp.float32), arrived[:, :components].reshape(n_...  5.65 us
    ppermute x1, starting transfers between devices, with_halo(): high = lax.ppermute(block, axis, backward)  5.48 us
  transfers between devices with their start and end apart: 5, of which 4 were waited for; matrix products, arithmetic and copies ran while one was open for 2% of the time, Pallas kernels for 0%

profile of v2, /device:TPU:1, one launch (start us, length us, event | category | flops | bytes accessed | tf_op | source)
XLA Modules:
  0.0 163.5 jit_solution(11892462363533184894)
XLA Ops:
  0.7 1.0 copy.33
  1.7 4.6 %collective-permute-start.1 = (f32[16,1,45,128]{3,2,0,1:T(8,128)S(1)}, f32[16,1,45,128]{3,2,0,1:T(8,128)S(1)}, u32[]{:S(2)}, u32[]{:S(2)}) collective-permute-start(f32[16,1,45,128]{3,2,0,1:T(8,128)S(1)} %copy.33), channel_id=1, source_target_pairs={{0,1},{1,2},{2,3},{3,4},{4,5},{5,6},{6,7},{7,8},{8,9},{9,10},{10,1... | collective-permute-start | bytes 1105928 | tf_op jit(solution)/shard_map/ppermute | solution.py:13
  6.3 5.5 %collective-permute-start = (f32[16,1,45,128]{3,2,0,1:T(8,128)S(1)}, f32[16,1,45,128]{3,2,0,1:T(8,128)S(1)}, u32[]{:S(2)}, u32[]{:S(2)}) collective-permute-start(f32[16,1,45,128]{3,2,0,1:T(8,128)S(1)} %copy.33), channel_id=1, source_target_pairs={{1,0},{2,1},{3,2},{4,3},{5,4},{6,5},{7,6},{8,7},{9,8},{10,9},{11,1... | collective-permute-start | bytes 1105928 | tf_op jit(solution)/shard_map/ppermute | solution.py:14
  11.8 3.6 %collective-permute-done = f32[16,1,45,128]{3,2,0,1:T(8,128)S(1)} collective-permute-done((f32[16,1,45,128]{3,2,0,1:T(8,128)S(1)}, f32[16,1,45,128]{3,2,0,1:T(8,128)S(1)}, u32[]{:S(2)}, u32[]{:S(2)}) %collective-permute-start) | collective-permute-done | bytes 368672 | tf_op jit(solution)/shard_map/ppermute | solution.py:14
  15.4 1.1 add_bitcast_fusion
  16.5 0.5 fusion.7
  17.0 0.1 reshape.119
  17.1 0.1 copy.55
  17.3 0.8 pad_maximum_fusion.1
  18.1 10.0 %all-to-all-start = ((f32[8,16,896]{2,1,0:T(8,128)}), f32[8,16,896]{2,1,0:T(8,128)S(1)}, u32[]{:S(2)}, u32[]{:S(2)}) async-start(f32[8,16,896]{2,1,0:T(8,128)} %pad_maximum_fusion.1), calls=%async_computation | async-start | bytes 917504 | tf_op jit(solution)/shard_map/all_to_all | solution.py:46
  28.8 0.2 convert_reduce_fusion
  29.0 0.1 iota_compare_fusion.2
  29.0 10.7 %all-to-all-done = f32[8,16,896]{2,1,0:T(8,128)S(1)} async-done(((f32[8,16,896]{2,1,0:T(8,128)}), f32[8,16,896]{2,1,0:T(8,128)S(1)}, u32[]{:S(2)}, u32[]{:S(2)}) %all-to-all-start) | async-done | bytes 458784 | tf_op jit(solution)/shard_map/all_to_all | solution.py:46
  39.7 1.2 fusion.5
  40.9 3.5 %all-to-all-start.1 = ((f32[8,16,768]{2,1,0:T(8,128)}), f32[8,16,768]{2,1,0:T(8,128)S(1)}, u32[]{:S(2)}, u32[]{:S(2)}) async-start(f32[8,16,768]{2,1,0:T(8,128)} %bitcast.6), calls=%async_computation.1 | async-start | bytes 786432 | tf_op jit(solution)/shard_map/all_to_all | solution.py:50
  44.4 0.1 select_reduce_fusion
  44.5 0.1 iota_compare_fusion.1
  44.6 0.2 and_reduce_fusion
  44.8 11.1 %all-to-all-done.1 = f32[8,16,768]{2,1,0:T(8,128)S(1)} async-done(((f32[8,16,768]{2,1,0:T(8,128)}), f32[8,16,768]{2,1,0:T(8,128)S(1)}, u32[]{:S(2)}, u32[]{:S(2)}) %all-to-all-start.1) | async-done | bytes 393248 | tf_op jit(solution)/shard_map/all_to_all | solution.py:50
  56.0 0.1 copy.37
  56.1 0.8 slice_bitcast_fusion
  56.9 1.4 fusion.9
  58.2 0.1 broadcast_in_dim.54
  58.3 0.4 pad_maximum_fusion
  58.7 3.4 %copy.40 = f32[128,46,128]{2,1,0:T(8,128)} copy(f32[128,46,128]{2,0,1:T(8,128)S(1)} %pad_maximum_fusion) | data formatting | bytes 6029312 | tf_op jit(solution)/shard_map/concatenate | solution.py:72
  62.1 17.5 %all-to-all-start.2 = ((f32[128,46,128]{2,1,0:T(8,128)}), f32[128,46,128]{2,1,0:T(8,128)S(1)}, u32[]{:S(2)}, u32[]{:S(2)}) async-start(f32[128,46,128]{2,1,0:T(8,128)} %copy.40), calls=%async_computation.2 | async-start | bytes 6291456 | tf_op jit(solution)/shard_map/all_to_all | solution.py:73
  79.6 2.1 %copy.42 = f32[16,1,45,128]{3,1,2,0:T(1,128)} copy(f32[16,1,45,128]{3,0,2,1:T(8,128)} %get-tuple-element.9) | data formatting | bytes 737280
  81.7 71.4 %all-to-all-done.2 = f32[128,46,128]{2,1,0:T(8,128)S(1)} async-done(((f32[128,46,128]{2,1,0:T(8,128)}), f32[128,46,128]{2,1,0:T(8,128)S(1)}, u32[]{:S(2)}, u32[]{:S(2)}) %all-to-all-start.2) | async-done | bytes 3014688 | tf_op jit(solution)/shard_map/all_to_all | solution.py:73
  153.1 2.4 %fusion.12 = s32[128]{0:T(128)S(1)} fusion(f32[128,46,128]{2,1,0:T(8,128)S(1)} %all-to-all-done.2), kind=kLoop, calls=%fused_computation.20 | loop fusion | flops 128 | bytes 1024 | tf_op jit(solution)/shard_map/convert_element_type | solution.py:75
  155.4 0.1 fusion.16
  155.5 2.3 %copy.43 = f32[128,45,128]{0,2,1:T(8,128)} copy(f32[128,45,128]{2,1,0:T(8,128)S(1)} %bitcast.58) | data formatting | bytes 5898240
  157.8 5.7 %fusion = f32[1,1,128,45,128]{4,2,3,1,0:T(8,128)} fusion(f32[128,45,128]{0,2,1:T(8,128)} %copy.43, bf16[1,1,128,45,128]{4,2,3,1,0:T(8,128)(2,1)} %param.11, pred[128]{0:T(512)(128)(4,1)S(1)} %fusion.16, s32[128]{0:T(128)S(1)} %fusion.12), kind=kOutput, calls=%fused_computation.2 | convolution fusion | flops 1133953024 | bytes 7373440 | tf_op jit(solution)/shard_map/dot_general | solution.py:78
  (16 shorter events, 0.1 us)
Async XLA Ops:
  0.6 15.9 %copy-start = (f32[1,128,128]{2,1,0:T(8,128)S(1)}, f32[1,128,128]{2,1,0:T(8,128)}, u32[]{:S(2)}) copy-start(f32[1,128,128]{2,1,0:T(8,128)} %param.10) | copy-start | bytes 196612
  0.6 16.6 %copy-start.1 = (f32[1,16,128]{2,1,0:T(8,128)S(1)}, f32[1,16,128]{2,1,0:T(8,128)}, u32[]{:S(2)}) copy-start(f32[1,16,128]{2,1,0:T(8,128)} %param.9) | copy-start | bytes 24580
  1.7 27.0 %copy-start.3 = (s32[1,1,64]{2,1,0:T(1,128)S(1)}, s32[1,1,64]{2,1,0:T(1,128)}, u32[]{:S(2)}) copy-start(s32[1,1,64]{2,1,0:T(1,128)} %param.13) | copy-start | bytes 772
  1.7 27.2 %copy-start.4 = (s32[1,1,64]{2,1,0:T(1,128)S(1)}, s32[1,1,64]{2,1,0:T(1,128)}, u32[]{:S(2)}) copy-start(s32[1,1,64]{2,1,0:T(1,128)} %param.14) | copy-start | bytes 772
  1.7 10.1 %collective-permute-start.1 = (f32[16,1,45,128]{3,2,0,1:T(8,128)S(1)}, f32[16,1,45,128]{3,2,0,1:T(8,128)S(1)}, u32[]{:S(2)}, u32[]{:S(2)}) collective-permute-start(f32[16,1,45,128]{3,2,0,1:T(8,128)S(1)} %copy.33), channel_id=1, source_target_pairs={{0,1},{1,2},{2,3},{3,4},{4,5},{5,6},{6,7},{7,8},{8,9},{9,10},{10,1... | collective-permute-start | bytes 1105928 | tf_op jit(solution)/shard_map/ppermute | solution.py:13
  6.3 9.1 %collective-permute-start = (f32[16,1,45,128]{3,2,0,1:T(8,128)S(1)}, f32[16,1,45,128]{3,2,0,1:T(8,128)S(1)}, u32[]{:S(2)}, u32[]{:S(2)}) collective-permute-start(f32[16,1,45,128]{3,2,0,1:T(8,128)S(1)} %copy.33), channel_id=1, source_target_pairs={{1,0},{2,1},{3,2},{4,3},{5,4},{6,5},{7,6},{8,7},{9,8},{10,9},{11,1... | collective-permute-start | bytes 1105928 | tf_op jit(solution)/shard_map/ppermute | solution.py:14
  16.5 28.0 %copy-start.2 = (s32[1,1,64]{2,1,0:T(1,128)S(1)}, s32[1,1,64]{2,1,0:T(1,128)}, u32[]{:S(2)}) copy-start(s32[1,1,64]{2,1,0:T(1,128)} %param.12) | copy-start | bytes 772
  18.1 21.7 %all-to-all-start = ((f32[8,16,896]{2,1,0:T(8,128)}), f32[8,16,896]{2,1,0:T(8,128)S(1)}, u32[]{:S(2)}, u32[]{:S(2)}) async-start(f32[8,16,896]{2,1,0:T(8,128)} %pad_maximum_fusion.1), calls=%async_computation | async-start | bytes 917504 | tf_op jit(solution)/shard_map/all_to_all | solution.py:46
  40.9 15.0 %all-to-all-start.1 = ((f32[8,16,768]{2,1,0:T(8,128)}), f32[8,16,768]{2,1,0:T(8,128)S(1)}, u32[]{:S(2)}, u32[]{:S(2)}) async-start(f32[8,16,768]{2,1,0:T(8,128)} %bitcast.6), calls=%async_computation.1 | async-start | bytes 786432 | tf_op jit(solution)/shard_map/all_to_all | solution.py:50
  62.1 91.0 %all-to-all-start.2 = ((f32[128,46,128]{2,1,0:T(8,128)}), f32[128,46,128]{2,1,0:T(8,128)S(1)}, u32[]{:S(2)}, u32[]{:S(2)}) async-start(f32[128,46,128]{2,1,0:T(8,128)} %copy.40), calls=%async_computation.2 | async-start | bytes 6291456 | tf_op jit(solution)/shard_map/all_to_all | solution.py:73

commit v3 on v2

--- a/solution.py
+++ b/solution.py
@@ -34,27 +34,9 @@
 
     low, high = with_halo(flux, "blk", 1)
     residual = 0.25 * high - 0.75 * low + 0.5 * flux
-    padded_q = -(-components // n_pitch) * n_pitch
-    chunk_q = padded_q // n_pitch
-    width = chunk_q * span_cells
     res = residual.reshape(pitch_local, components, span_cells)
-    res = jnp.pad(res, ((0, 0), (0, padded_q - components), (0, 0)))
-    spanned = jnp.einsum("pqs,ts->pqt", res, span_inverse[0], precision=highest)
-    chunks = spanned.reshape(pitch_local, n_pitch, width).transpose(1, 0, 2)
-    pinv_rows = jnp.broadcast_to(pitch_inverse[0][None], (n_pitch,) + pitch_inverse.shape[1:])
-    chunks = jnp.concatenate([chunks, pinv_rows], axis=2)
-    gathered = lax.all_to_all(chunks, "pitch", 0, 0, tiled=True)
-    gathered = gathered.reshape(n_pitch * pitch_local, width + pitch_inverse.shape[2])
-    pinv_full = gathered[:, width:]
-    mixed = jnp.dot(pinv_full, gathered[:, :width], precision=highest)
-    back = lax.all_to_all(mixed.reshape(n_pitch, pitch_local, width), "pitch", 0, 0, tiled=True)
-    smoothed = (
-        back.reshape(n_pitch, pitch_local, chunk_q, span_cells)
-        .transpose(1, 0, 2, 3)
-        .reshape(pitch_local, padded_q, span_cells)[:, :components]
-    )
+    spanned_all = jnp.einsum("pqs,ts->pqt", res, span_inverse[0], precision=highest)
 
-    rows = smoothed.reshape(pitch_local * axial_local, components * span_cells)
     my_owner = send_owner[0, 0]
     live = jnp.arange(entries, dtype=jnp.int32) < send_count[0, 0]
     target = jnp.where(live, my_owner * CAP + entry_ranks(my_owner), -1)
@@ -65,19 +47,55 @@
         hits[:, :, None] & (send_row[0, 0][None, :, None] == row_ids[None, None, :]), axis=1
     ).astype(jnp.float32)
     tag = jnp.sum(jnp.where(hits, send_slot[0, 0][None, :] + 1, 0), axis=1) - 1
-    outgoing = jnp.dot(select_out, rows, precision=highest).reshape(
-        n_blk * CAP, components, span_cells
-    )
     tag_row = jnp.broadcast_to(tag.astype(jnp.float32)[:, None, None], (n_blk * CAP, 1, span_cells))
-    outgoing = jnp.concatenate([outgoing, tag_row], axis=1)
-    arrived = lax.all_to_all(outgoing, "blk", 0, 0, tiled=True)
 
-    arrived_slot = arrived[:, components, 0].astype(jnp.int32)
+    halves = 2
+    per_chunk = -(-components // (halves * n_pitch))
+    pinv_full = None
+    smoothed_parts, arrived_parts = [], []
+    for half in range(halves):
+        q0 = half * per_chunk * n_pitch
+        q1 = min(components, q0 + per_chunk * n_pitch)
+        width = per_chunk * span_cells
+        part = spanned_all[:, q0:q1]
+        part = jnp.pad(part, ((0, 0), (0, per_chunk * n_pitch - (q1 - q0)), (0, 0)))
+        chunks = part.reshape(pitch_local, n_pitch, width).transpose(1, 0, 2)
+        if pinv_full is None:
+            pinv_rows = jnp.broadcast_to(
+                pitch_inverse[0][None], (n_pitch,) + pitch_inverse.shape[1:]
+            )
+            chunks = jnp.concatenate([chunks, pinv_rows], axis=2)
+        gathered = lax.all_to_all(chunks, "pitch", 0, 0, tiled=True)
+        gathered = gathered.reshape(n_pitch * pitch_local, gathered.shape[2])
+        if pinv_full is None:
+            pinv_full = gathered[:, width:]
+        mixed = jnp.dot(pinv_full, gathered[:, :width], precision=highest)
+        back = lax.all_to_all(
+            mixed.reshape(n_pitch, pitch_local, width), "pitch", 0, 0, tiled=True
+        )
+        smooth_part = (
+            back.reshape(n_pitch, pitch_local, per_chunk, span_cells)
+            .transpose(1, 0, 2, 3)
+            .reshape(pitch_local, per_chunk * n_pitch, span_cells)[:, : q1 - q0]
+        )
+        smoothed_parts.append(smooth_part)
+        outgoing = jnp.dot(
+            select_out, smooth_part.reshape(pitch_local, (q1 - q0) * span_cells), precision=highest
+        ).reshape(n_blk * CAP, q1 - q0, span_cells)
+        if half == 0:
+            outgoing = jnp.concatenate([outgoing, tag_row], axis=1)
+        arrived_parts.append(lax.all_to_all(outgoing, "blk", 0, 0, tiled=True))
+
+    smoothed = jnp.concatenate(smoothed_parts, axis=1)
+    first = arrived_parts[0]
+    head_q = first.shape[1] - 1
+    arrived_slot = first[:, head_q, 0].astype(jnp.int32)
+    arrived = jnp.concatenate([first[:, :head_q]] + arrived_parts[1:], axis=1)
     select_in = arrived_slot[None, :] == jnp.arange(slot_total, dtype=jnp.int32)[:, None]
     filled = jnp.any(select_in, axis=1)
     incoming = jnp.dot(
         select_in.astype(jnp.float32),
-        arrived[:, :components].reshape(n_blk * CAP, components * span_cells),
+        arrived.reshape(n_blk * CAP, components * span_cells),
         precision=highest,
     ).reshape(slot_total, components, span_cells)
     storage = jnp.where(filled[:, None, None], incoming, store_old[0, 0].astype(jnp.float32))

time: 164 us -> 202 us (1.23)
  waiting for transfers between devices: 96.8 us -> 118 us
  starting transfers between devices: 41.1 us -> 51.4 us
  local copies, waits for them, and re-layouts: 10.1 us -> 15.1 us
    all_to_all x1 -> x2, waiting for transfers between devices: 71.4 us -> 84.2 us  [local(): arrived_parts.append(lax.all_to_all(outgoing, 'blk', 0, 0, tiled=True))]
    all_to_all x1 -> x2, waiting for transfers between devices: 10.7 us -> 16 us  [local(): gathered = lax.all_to_all(chunks, 'pitch', 0, 0, tiled=True)]
    all_to_all x1 -> x2, starting transfers between devices: 17.5 us -> 21.1 us  [local(): arrived_parts.append(lax.all_to_all(outgoing, 'blk', 0, 0, tiled=True))]
    all_to_all x1 -> x2, waiting for transfers between devices: 11.1 us -> 14.7 us  [local(): lax.all_to_all(mixed.reshape(n_pitch, pitch_local, width), 'pitch', 0, 0,...]
    all_to_all x1 -> x2, starting transfers between devices: 10 us -> 13.4 us  [local(): gathered = lax.all_to_all(chunks, 'pitch', 0, 0, tiled=True)]
    all_to_all x1 -> x2, starting transfers between devices: 3.45 us -> 6.78 us  [local(): lax.all_to_all(mixed.reshape(n_pitch, pitch_local, width), 'pitch', 0, 0,...]
    unnamed x14 -> x16, local copies, waits for them, and re-layouts: 6.27 us -> 6.41 us
    dot_general x3 -> x4, matrix products: 7.48 us -> 7.35 us  [the longest x1 5.27 us: local(): jnp.dot(select_in.astype(jnp.float32), arrived.reshape(n_blk * CAP, compo...]
  transfers between devices with their start and end apart: 5 -> 8, of which waited for: 4 -> 7; matrix products, arithmetic and copies ran while one was open for 2% -> 6% of each run, Pallas kernels for 0% -> 0%
where the time goes in v3:
time: 202 us; the launch traced here: 201 us
  waiting for transfers between devices  118 us (58%)
  starting transfers between devices  51.4 us (25%)
  local copies, waits for them, and re-layouts  15.1 us (7%)
  matrix products  9.34 us (5%)
  other arithmetic  5.09 us (3%)
    all_to_all x2, waiting for transfers between devices, local(): arrived_parts.append(lax.all_to_all(outgoing, 'blk', 0, 0, tiled=True))  84.2 us
    all_to_all x2, starting transfers between devices, local(): arrived_parts.append(lax.all_to_all(outgoing, 'blk', 0, 0, tiled=True))  21.1 us
    all_to_all x2, waiting for transfers between devices, local(): gathered = lax.all_to_all(chunks, 'pitch', 0, 0, tiled=True)  16 us
    all_to_all x2, waiting for transfers between devices, local(): lax.all_to_all(mixed.reshape(n_pitch, pitch_local, width), 'pitch', 0, 0,...  14.7 us
    all_to_all x2, starting transfers between devices, local(): gathered = lax.all_to_all(chunks, 'pitch', 0, 0, tiled=True)  13.4 us
    all_to_all x2, starting transfers between devices, local(): lax.all_to_all(mixed.reshape(n_pitch, pitch_local, width), 'pitch', 0, 0,...  6.78 us
    unnamed x16, local copies, waits for them, and re-layouts  6.41 us
    ppermute x1, starting transfers between devices, with_halo(): high = lax.ppermute(block, axis, backward)  5.48 us
  transfers between devices with their start and end apart: 8, of which 7 were waited for; matrix products, arithmetic and copies ran while one was open for 6% of the time, Pallas kernels for 0%

profile of v3, /device:TPU:1, one launch (start us, length us, event | category | flops | bytes accessed | tf_op | source)
XLA Modules:
  0.0 200.8 jit_solution(12453241182354104722)
XLA Ops:
  0.6 1.0 copy.44
  1.7 4.6 %collective-permute-start.1 = (f32[16,1,45,128]{3,0,2,1:T(8,128)S(1)}, f32[16,1,45,128]{3,0,2,1:T(8,128)S(1)}, u32[]{:S(2)}, u32[]{:S(2)}) collective-permute-start(f32[16,1,45,128]{3,0,2,1:T(8,128)S(1)} %copy.44), channel_id=1, source_target_pairs={{0,1},{1,2},{2,3},{3,4},{4,5},{5,6},{6,7},{7,8},{8,9},{9,10},{10,1... | collective-permute-start | bytes 1105928 | tf_op jit(solution)/shard_map/ppermute | solution.py:13
  6.3 5.5 %collective-permute-start = (f32[16,1,45,128]{3,0,2,1:T(8,128)S(1)}, f32[16,1,45,128]{3,0,2,1:T(8,128)S(1)}, u32[]{:S(2)}, u32[]{:S(2)}) collective-permute-start(f32[16,1,45,128]{3,0,2,1:T(8,128)S(1)} %copy.44), channel_id=1, source_target_pairs={{1,0},{2,1},{3,2},{4,3},{5,4},{6,5},{7,6},{8,7},{9,8},{10,9},{11,1... | collective-permute-start | bytes 1105928 | tf_op jit(solution)/shard_map/ppermute | solution.py:14
  11.8 3.3 %collective-permute-done = f32[16,1,45,128]{3,0,2,1:T(8,128)S(1)} collective-permute-done((f32[16,1,45,128]{3,0,2,1:T(8,128)S(1)}, f32[16,1,45,128]{3,0,2,1:T(8,128)S(1)}, u32[]{:S(2)}, u32[]{:S(2)}) %collective-permute-start) | collective-permute-done | bytes 368672 | tf_op jit(solution)/shard_map/ppermute | solution.py:14
  15.1 1.1 add_bitcast_fusion
  16.9 0.7 pad_maximum_fusion.1
  17.6 10.0 %all-to-all-start = ((f32[8,16,512]{2,1,0:T(8,128)}), f32[8,16,512]{2,1,0:T(8,128)S(1)}, u32[]{:S(2)}, u32[]{:S(2)}) async-start(f32[8,16,512]{2,1,0:T(8,128)} %pad_maximum_fusion.1), calls=%async_computation | async-start | bytes 524288 | tf_op jit(solution)/shard_map/all_to_all | solution.py:68
  28.6 0.7 copy.81
  29.3 7.7 %all-to-all-done = f32[8,16,512]{2,1,0:T(8,128)S(1)} async-done(((f32[8,16,512]{2,1,0:T(8,128)}), f32[8,16,512]{2,1,0:T(8,128)S(1)}, u32[]{:S(2)}, u32[]{:S(2)}) %all-to-all-start) | async-done | bytes 262176 | tf_op jit(solution)/shard_map/all_to_all | solution.py:68
  37.0 3.4 %all-to-all-start.2 = ((f32[8,16,384]{2,1,0:T(8,128)}), f32[8,16,384]{2,1,0:T(8,128)S(1)}, u32[]{:S(2)}, u32[]{:S(2)}) async-start(f32[8,16,384]{2,1,0:T(8,128)} %bitcast.75), calls=%async_computation.2 | async-start | bytes 393216 | tf_op jit(solution)/shard_map/all_to_all | solution.py:68
  40.6 8.4 %all-to-all-done.2 = f32[8,16,384]{2,1,0:T(8,128)S(1)} async-done(((f32[8,16,384]{2,1,0:T(8,128)}), f32[8,16,384]{2,1,0:T(8,128)S(1)}, u32[]{:S(2)}, u32[]{:S(2)}) %all-to-all-start.2) | async-done | bytes 196640 | tf_op jit(solution)/shard_map/all_to_all | solution.py:68
  49.0 1.0 fusion.25
  49.9 3.4 %all-to-all-start.3 = ((f32[8,16,384]{2,1,0:T(8,128)}), f32[8,16,384]{2,1,0:T(8,128)S(1)}, u32[]{:S(2)}, u32[]{:S(2)}) async-start(f32[8,16,384]{2,1,0:T(8,128)} %fusion.25), calls=%async_computation.3 | async-start | bytes 393216 | tf_op jit(solution)/shard_map/all_to_all | solution.py:73
  53.6 1.0 fusion.9
  54.5 7.4 %all-to-all-done.3 = f32[8,16,384]{2,1,0:T(8,128)S(1)} async-done(((f32[8,16,384]{2,1,0:T(8,128)}), f32[8,16,384]{2,1,0:T(8,128)S(1)}, u32[]{:S(2)}, u32[]{:S(2)}) %all-to-all-start.3) | async-done | bytes 196640 | tf_op jit(solution)/shard_map/all_to_all | solution.py:73
  62.0 3.4 %all-to-all-start.1 = ((f32[8,16,384]{2,1,0:T(8,128)}), f32[8,16,384]{2,1,0:T(8,128)S(1)}, u32[]{:S(2)}, u32[]{:S(2)}) async-start(f32[8,16,384]{2,1,0:T(8,128)} %bitcast.6), calls=%async_computation.1 | async-start | bytes 393216 | tf_op jit(solution)/shard_map/all_to_all | solution.py:73
  65.5 0.7 fusion.11
  66.3 2.0 copy.58
  68.3 7.2 %all-to-all-done.1 = f32[8,16,384]{2,1,0:T(8,128)S(1)} async-done(((f32[8,16,384]{2,1,0:T(8,128)}), f32[8,16,384]{2,1,0:T(8,128)S(1)}, u32[]{:S(2)}, u32[]{:S(2)}) %all-to-all-start.1) | async-done | bytes 196640 | tf_op jit(solution)/shard_map/all_to_all | solution.py:73
  75.5 15.0 %all-to-all-start.5 = ((f32[128,21,128]{2,1,0:T(8,128)}), f32[128,21,128]{2,1,0:T(8,128)S(1)}, u32[]{:S(2)}, u32[]{:S(2)}) async-start(f32[128,21,128]{2,1,0:T(8,128)} %copy.58), calls=%async_computation.5 | async-start | bytes 3145728 | tf_op jit(solution)/shard_map/all_to_all | solution.py:87
  90.9 0.8 fusion.6
  92.0 2.3 %copy.54 = f32[128,25,128]{2,1,0:T(8,128)} copy(f32[128,25,128]{2,0,1:T(8,128)S(1)} %pad_maximum_fusion) | data formatting | bytes 3276800 | tf_op jit(solution)/shard_map/concatenate | solution.py:86
  94.3 36.0 %all-to-all-done.5 = f32[128,21,128]{2,1,0:T(8,128)S(1)} async-done(((f32[128,21,128]{2,1,0:T(8,128)}), f32[128,21,128]{2,1,0:T(8,128)S(1)}, u32[]{:S(2)}, u32[]{:S(2)}) %all-to-all-start.5) | async-done | bytes 1376288 | tf_op jit(solution)/shard_map/all_to_all | solution.py:87
  130.3 1.2 copy-done.1
  131.4 6.1 %all-to-all-start.4 = ((f32[128,25,128]{2,1,0:T(8,128)}), f32[128,25,128]{2,1,0:T(8,128)S(1)}, u32[]{:S(2)}, u32[]{:S(2)}) async-start(f32[128,25,128]{2,1,0:T(8,128)} %copy.54), calls=%async_computation.4 | async-start | bytes 4194304 | tf_op jit(solution)/shard_map/all_to_all | solution.py:87
  137.6 1.1 copy.60
  138.7 1.8 copy.59
  140.6 48.2 %all-to-all-done.4 = f32[128,25,128]{2,1,0:T(8,128)S(1)} async-done(((f32[128,25,128]{2,1,0:T(8,128)}), f32[128,25,128]{2,1,0:T(8,128)S(1)}, u32[]{:S(2)}, u32[]{:S(2)}) %all-to-all-start.4) | async-done | bytes 1638432 | tf_op jit(solution)/shard_map/all_to_all | solution.py:87
  188.7 1.3 slice.34
  190.0 3.0 %copy.61 = f32[128,24,128]{0,2,1:T(8,128)} copy(f32[128,24,128]{2,1,0:T(8,128)} %slice.34) | data formatting | bytes 3145728
  193.1 2.4 %fusion.14 = s32[128]{0:T(128)S(1)} fusion(f32[128,25,128]{2,1,0:T(8,128)S(1)} %all-to-all-done.4), kind=kLoop, calls=%fused_computation.25 | loop fusion | flops 128 | bytes 1024 | tf_op jit(solution)/shard_map/convert_element_type | solution.py:92
  195.5 5.3 %fusion.3 = f32[1,1,128,45,128]{4,2,3,1,0:T(8,128)} fusion(f32[128,21,128]{0,2,1:T(8,128)S(1)} %copy.59, f32[128,24,128]{0,2,1:T(8,128)} %copy.61, bf16[1,1,128,45,128]{4,2,3,1,0:T(8,128)(2,1)} %param.11, pred[128]{0:T(512)(128)(4,1)S(1)} %fusion.17, s32[128]{0:T(128)S(1)} %fusion.14), kind=kOutput, calls=%fused_computation.5 | convolution fusion | flops 1134690304 | bytes 7373440 | tf_op jit(solution)/shard_map/dot_general | solution.py:96
  (40 shorter events, 2.2 us)
Async XLA Ops:
  0.6 15.6 %copy-start = (f32[1,128,128]{2,1,0:T(8,128)S(1)}, f32[1,128,128]{2,1,0:T(8,128)}, u32[]{:S(2)}) copy-start(f32[1,128,128]{2,1,0:T(8,128)} %param.10) | copy-start | bytes 196612
  1.7 15.2 %copy-start.2 = (f32[1,16,128]{2,1,0:T(8,128)S(1)}, f32[1,16,128]{2,1,0:T(8,128)}, u32[]{:S(2)}) copy-start(f32[1,16,128]{2,1,0:T(8,128)} %param.9) | copy-start | bytes 24580
  1.7 10.1 %collective-permute-start.1 = (f32[16,1,45,128]{3,0,2,1:T(8,128)S(1)}, f32[16,1,45,128]{3,0,2,1:T(8,128)S(1)}, u32[]{:S(2)}, u32[]{:S(2)}) collective-permute-start(f32[16,1,45,128]{3,0,2,1:T(8,128)S(1)} %copy.44), channel_id=1, source_target_pairs={{0,1},{1,2},{2,3},{3,4},{4,5},{5,6},{6,7},{7,8},{8,9},{9,10},{10,1... | collective-permute-start | bytes 1105928 | tf_op jit(solution)/shard_map/ppermute | solution.py:13
  6.3 8.8 %collective-permute-start = (f32[16,1,45,128]{3,0,2,1:T(8,128)S(1)}, f32[16,1,45,128]{3,0,2,1:T(8,128)S(1)}, u32[]{:S(2)}, u32[]{:S(2)}) collective-permute-start(f32[16,1,45,128]{3,0,2,1:T(8,128)S(1)} %copy.44), channel_id=1, source_target_pairs={{1,0},{2,1},{3,2},{4,3},{5,4},{6,5},{7,6},{8,7},{9,8},{10,9},{11,1... | collective-permute-start | bytes 1105928 | tf_op jit(solution)/shard_map/ppermute | solution.py:14
  16.2 12.1 %copy-start.4 = (s32[1,1,64]{2,1,0:T(1,128)S(1)}, s32[1,1,64]{2,1,0:T(1,128)}, u32[]{:S(2)}) copy-start(s32[1,1,64]{2,1,0:T(1,128)} %param.13) | copy-start | bytes 772
  16.9 23.6 %copy-start.3 = (s32[1,1,64]{2,1,0:T(1,128)S(1)}, s32[1,1,64]{2,1,0:T(1,128)}, u32[]{:S(2)}) copy-start(s32[1,1,64]{2,1,0:T(1,128)} %param.12) | copy-start | bytes 772
  17.6 19.4 %all-to-all-start = ((f32[8,16,512]{2,1,0:T(8,128)}), f32[8,16,512]{2,1,0:T(8,128)S(1)}, u32[]{:S(2)}, u32[]{:S(2)}) async-start(f32[8,16,512]{2,1,0:T(8,128)} %pad_maximum_fusion.1), calls=%async_computation | async-start | bytes 524288 | tf_op jit(solution)/shard_map/all_to_all | solution.py:68
  37.0 12.0 %all-to-all-start.2 = ((f32[8,16,384]{2,1,0:T(8,128)}), f32[8,16,384]{2,1,0:T(8,128)S(1)}, u32[]{:S(2)}, u32[]{:S(2)}) async-start(f32[8,16,384]{2,1,0:T(8,128)} %bitcast.75), calls=%async_computation.2 | async-start | bytes 393216 | tf_op jit(solution)/shard_map/all_to_all | solution.py:68
  49.9 12.0 %all-to-all-start.3 = ((f32[8,16,384]{2,1,0:T(8,128)}), f32[8,16,384]{2,1,0:T(8,128)S(1)}, u32[]{:S(2)}, u32[]{:S(2)}) async-start(f32[8,16,384]{2,1,0:T(8,128)} %fusion.25), calls=%async_computation.3 | async-start | bytes 393216 | tf_op jit(solution)/shard_map/all_to_all | solution.py:73
  62.0 13.5 %all-to-all-start.1 = ((f32[8,16,384]{2,1,0:T(8,128)}), f32[8,16,384]{2,1,0:T(8,128)S(1)}, u32[]{:S(2)}, u32[]{:S(2)}) async-start(f32[8,16,384]{2,1,0:T(8,128)} %bitcast.6), calls=%async_computation.1 | async-start | bytes 393216 | tf_op jit(solution)/shard_map/all_to_all | solution.py:73
  68.3 22.3 %copy-start.5 = (s32[1,1,64]{2,1,0:T(1,128)S(1)}, s32[1,1,64]{2,1,0:T(1,128)}, u32[]{:S(2)}) copy-start(s32[1,1,64]{2,1,0:T(1,128)} %param.14) | copy-start | bytes 772
  75.5 54.8 %all-to-all-start.5 = ((f32[128,21,128]{2,1,0:T(8,128)}), f32[128,21,128]{2,1,0:T(8,128)S(1)}, u32[]{:S(2)}, u32[]{:S(2)}) async-start(f32[128,21,128]{2,1,0:T(8,128)} %copy.58), calls=%async_computation.5 | async-start | bytes 3145728 | tf_op jit(solution)/shard_map/all_to_all | solution.py:87
  130.3 1.2 copy-start.1
  131.4 57.3 %all-to-all-start.4 = ((f32[128,25,128]{2,1,0:T(8,128)}), f32[128,25,128]{2,1,0:T(8,128)S(1)}, u32[]{:S(2)}, u32[]{:S(2)}) async-start(f32[128,25,128]{2,1,0:T(8,128)} %copy.54), calls=%async_computation.4 | async-start | bytes 4194304 | tf_op jit(solution)/shard_map/all_to_all | solution.py:87

commit v4 on v2

--- a/solution.py
+++ b/solution.py
@@ -65,22 +65,20 @@
         hits[:, :, None] & (send_row[0, 0][None, :, None] == row_ids[None, None, :]), axis=1
     ).astype(jnp.float32)
     tag = jnp.sum(jnp.where(hits, send_slot[0, 0][None, :] + 1, 0), axis=1) - 1
-    outgoing = jnp.dot(select_out, rows, precision=highest).reshape(
-        n_blk * CAP, components, span_cells
-    )
-    tag_row = jnp.broadcast_to(tag.astype(jnp.float32)[:, None, None], (n_blk * CAP, 1, span_cells))
-    outgoing = jnp.concatenate([outgoing, tag_row], axis=1)
-    arrived = lax.all_to_all(outgoing, "blk", 0, 0, tiled=True)
+    rows_ext = jnp.pad(smoothed.transpose(1, 0, 2), ((0, 1), (0, 1), (0, 0)))
+    rows_ext = rows_ext.at[components, pitch_local * axial_local].set(1.0)
+    select_ext = jnp.concatenate([select_out, tag.astype(jnp.float32)[:, None]], axis=1)
+    outgoing = jnp.einsum("qpt,sp->sqt", rows_ext, select_ext, precision=highest).transpose(1, 0, 2)
+    arrived = lax.all_to_all(outgoing, "blk", 1, 1, tiled=True)
 
-    arrived_slot = arrived[:, components, 0].astype(jnp.int32)
+    arrived_slot = arrived[components, :, 0].astype(jnp.int32)
     select_in = arrived_slot[None, :] == jnp.arange(slot_total, dtype=jnp.int32)[:, None]
     filled = jnp.any(select_in, axis=1)
-    incoming = jnp.dot(
-        select_in.astype(jnp.float32),
-        arrived[:, :components].reshape(n_blk * CAP, components * span_cells),
-        precision=highest,
-    ).reshape(slot_total, components, span_cells)
-    storage = jnp.where(filled[:, None, None], incoming, store_old[0, 0].astype(jnp.float32))
+    incoming = jnp.einsum(
+        "si,qit->qst", select_in.astype(jnp.float32), arrived[:components], precision=highest
+    )
+    old_t = store_old[0, 0].transpose(1, 0, 2).astype(jnp.float32)
+    storage = jnp.where(filled[None, :, None], incoming, old_t).transpose(1, 0, 2)
     return (smoothed.reshape(flux.shape), storage[None, None])
 
 

time: 164 us -> 162 us (0.988)
  local copies, waits for them, and re-layouts: 10.1 us -> 7.82 us
    transpose x0 -> x2, local copies, waits for them, and re-layouts: none -> 4.21 us  [the longest x1 3.42 us: local(): jnp.einsum('qpt,sp->sqt', rows_ext, select_ext, precision=highest)]
    concatenate x1 -> x0, local copies, waits for them, and re-layouts: 3.43 us -> none  [local(): outgoing = jnp.concatenate([outgoing, tag_row], axis=1)]
    unnamed x14 -> x12, local copies, waits for them, and re-layouts: 6.27 us -> 3.19 us
where the time goes in v4:
time: 162 us
  waiting for transfers between devices  96.8 us (60%)
  starting transfers between devices  41.1 us (25%)
  matrix products  9.75 us (6%)
  local copies, waits for them, and re-layouts  7.82 us (5%)
  other arithmetic  5 us (3%)
    all_to_all x1, waiting for transfers between devices, local(): arrived = lax.all_to_all(outgoing, 'blk', 1, 1, tiled=True)  71.4 us
    all_to_all x1, starting transfers between devices, local(): arrived = lax.all_to_all(outgoing, 'blk', 1, 1, tiled=True)  17.5 us
    all_to_all x1, waiting for transfers between devices, local(): lax.all_to_all(mixed.reshape(n_pitch, pitch_local, width), 'pitch', 0, 0,...  11.2 us
    all_to_all x1, waiting for transfers between devices, local(): gathered = lax.all_to_all(chunks, 'pitch', 0, 0, tiled=True)  10.6 us
    all_to_all x1, starting transfers between devices, local(): gathered = lax.all_to_all(chunks, 'pitch', 0, 0, tiled=True)  10 us
    dot_general x1, matrix products, local(): jnp.einsum('si,qit->qst', select_in.astype(jnp.float32), arrived[:compone...  5.49 us
    ppermute x1, starting transfers between devices, with_halo(): high = lax.ppermute(block, axis, backward)  5.48 us
    ppermute x1, starting transfers between devices, with_halo(): low = lax.ppermute(block, axis, forward)  4.58 us
  transfers between devices with their start and end apart: 5, of which 4 were waited for; matrix products, arithmetic and copies ran while one was open for 2% of the time, Pallas kernels for 0%

profile of v4, /device:TPU:1, one launch (start us, length us, event | category | flops | bytes accessed | tf_op | source)
XLA Modules:
  0.0 161.9 jit_solution(18241446567476415412)
XLA Ops:
  0.6 0.0 copy-start
  0.7 1.0 copy.29
  1.7 0.0 copy-start.3
  1.7 4.6 %collective-permute-start.1 = (f32[16,1,45,128]{3,2,0,1:T(8,128)S(1)}, f32[16,1,45,128]{3,2,0,1:T(8,128)S(1)}, u32[]{:S(2)}, u32[]{:S(2)}) collective-permute-start(f32[16,1,45,128]{3,2,0,1:T(8,128)S(1)} %copy.29), channel_id=1, source_target_pairs={{0,1},{1,2},{2,3},{3,4},{4,5},{5,6},{6,7},{7,8},{8,9},{9,10},{10,1... | collective-permute-start | bytes 1105928 | tf_op jit(solution)/shard_map/ppermute | solution.py:13
  6.3 5.5 %collective-permute-start = (f32[16,1,45,128]{3,2,0,1:T(8,128)S(1)}, f32[16,1,45,128]{3,2,0,1:T(8,128)S(1)}, u32[]{:S(2)}, u32[]{:S(2)}) collective-permute-start(f32[16,1,45,128]{3,2,0,1:T(8,128)S(1)} %copy.29), channel_id=1, source_target_pairs={{1,0},{2,1},{3,2},{4,3},{5,4},{6,5},{7,6},{8,7},{9,8},{10,9},{11,1... | collective-permute-start | bytes 1105928 | tf_op jit(solution)/shard_map/ppermute | solution.py:14
  11.8 3.6 %collective-permute-done = f32[16,1,45,128]{3,2,0,1:T(8,128)S(1)} collective-permute-done((f32[16,1,45,128]{3,2,0,1:T(8,128)S(1)}, f32[16,1,45,128]{3,2,0,1:T(8,128)S(1)}, u32[]{:S(2)}, u32[]{:S(2)}) %collective-permute-start) | collective-permute-done | bytes 368672 | tf_op jit(solution)/shard_map/ppermute | solution.py:14
  15.4 1.1 add_bitcast_fusion
  16.5 0.5 fusion.7
  17.0 0.1 reshape.145
  17.1 0.1 copy.44
  17.3 0.8 pad_maximum_fusion
  18.1 10.0 %all-to-all-start = ((f32[8,16,896]{2,1,0:T(8,128)}), f32[8,16,896]{2,1,0:T(8,128)S(1)}, u32[]{:S(2)}, u32[]{:S(2)}) async-start(f32[8,16,896]{2,1,0:T(8,128)} %pad_maximum_fusion), calls=%async_computation | async-start | bytes 917504 | tf_op jit(solution)/shard_map/all_to_all | solution.py:46
  28.8 0.2 convert_reduce_fusion
  28.9 0.1 iota_compare_fusion.2
  29.0 0.1 iota_compare_fusion.1
  29.1 10.6 %all-to-all-done = f32[8,16,896]{2,1,0:T(8,128)S(1)} async-done(((f32[8,16,896]{2,1,0:T(8,128)}), f32[8,16,896]{2,1,0:T(8,128)S(1)}, u32[]{:S(2)}, u32[]{:S(2)}) %all-to-all-start) | async-done | bytes 458784 | tf_op jit(solution)/shard_map/all_to_all | solution.py:46
  39.7 1.2 fusion.5
  40.9 3.5 %all-to-all-start.1 = ((f32[8,16,768]{2,1,0:T(8,128)}), f32[8,16,768]{2,1,0:T(8,128)S(1)}, u32[]{:S(2)}, u32[]{:S(2)}) async-start(f32[8,16,768]{2,1,0:T(8,128)} %bitcast.6), calls=%async_computation.1 | async-start | bytes 786432 | tf_op jit(solution)/shard_map/all_to_all | solution.py:50
  44.4 0.2 and_reduce_fusion
  44.6 0.1 select_reduce_fusion
  44.8 11.2 %all-to-all-done.1 = f32[8,16,768]{2,1,0:T(8,128)S(1)} async-done(((f32[8,16,768]{2,1,0:T(8,128)}), f32[8,16,768]{2,1,0:T(8,128)S(1)}, u32[]{:S(2)}, u32[]{:S(2)}) %all-to-all-start.1) | async-done | bytes 393248 | tf_op jit(solution)/shard_map/all_to_all | solution.py:50
  55.9 0.1 reshape.148
  56.0 0.1 copy.33
  56.1 0.8 slice_bitcast_fusion
  57.0 2.6 %convolution_bitcast_fusion = f32[46,128,128]{2,1,0:T(8,128)S(1)} fusion(f32[46,17,128]{2,1,0:T(8,128)S(1)} %scatter.4, f32[128,1]{0,1:T(1,128)S(1)} %convert_bitcast_fusion, f32[128,16]{0,1:T(8,128)S(1)} %convert_element_type.42), kind=kOutput, calls=%fused_computation.4 | convolution fusion | flops 153749632 | bytes 3423744 | tf_op jit(solution)/shard_map/qpt,sp->sqt/dot_general | solution.py:71
  59.5 3.4 %copy.34 = f32[46,128,128]{2,0,1:T(8,128)} copy(f32[46,128,128]{2,1,0:T(8,128)S(1)} %convolution_bitcast_fusion) | data formatting | bytes 6029312 | tf_op jit(solution)/shard_map/transpose | solution.py:71
  62.9 17.5 %all-to-all-start.2 = ((f32[46,128,128]{2,0,1:T(8,128)}), f32[46,128,128]{2,0,1:T(8,128)S(1)}, u32[]{:S(2)}, u32[]{:S(2)}) async-start(f32[46,128,128]{2,0,1:T(8,128)} %copy.34), calls=%async_computation.2 | async-start | bytes 6291456 | tf_op jit(solution)/shard_map/all_to_all | solution.py:72
  80.5 2.1 %copy.36 = f32[16,1,45,128]{3,1,2,0:T(1,128)} copy(f32[16,1,45,128]{3,0,2,1:T(8,128)} %get-tuple-element.21) | data formatting | bytes 737280
  82.6 71.4 %all-to-all-done.2 = f32[46,128,128]{2,0,1:T(8,128)S(1)} async-done(((f32[46,128,128]{2,0,1:T(8,128)}), f32[46,128,128]{2,0,1:T(8,128)S(1)}, u32[]{:S(2)}, u32[]{:S(2)}) %all-to-all-start.2) | async-done | bytes 3014688 | tf_op jit(solution)/shard_map/all_to_all | solution.py:72
  153.9 2.4 %fusion.9 = s32[128]{0:T(128)S(1)} fusion(f32[46,128,128]{2,0,1:T(8,128)S(1)} %all-to-all-done.2), kind=kLoop, calls=%fused_computation.16 | loop fusion | flops 128 | bytes 1024 | tf_op jit(solution)/shard_map/convert_element_type | solution.py:74
  156.3 0.1 fusion.13
  156.4 5.5 %fusion.2 = f32[1,1,128,45,128]{4,2,3,1,0:T(8,128)} fusion(f32[45,128,128]{2,0,1:T(8,128)S(1)} %bitcast.42, bf16[1,1,128,45,128]{4,2,3,1,0:T(8,128)(2,1)} %param.13, pred[128]{0:T(512)(128)(4,1)S(1)} %fusion.13, s32[128]{0:T(128)S(1)} %fusion.9), kind=kOutput, calls=%fused_computation.3 | convolution fusion | flops 1133953024 | bytes 7373440 | tf_op jit(solution)/shard_map/si,qit->qst/dot_general | solution.py:77
  (17 shorter events, 0.1 us)
Async XLA Ops:
  0.6 15.9 %copy-start = (f32[1,128,128]{2,1,0:T(8,128)S(1)}, f32[1,128,128]{2,1,0:T(8,128)}, u32[]{:S(2)}) copy-start(f32[1,128,128]{2,1,0:T(8,128)} %param.12) | copy-start | bytes 196612
  0.6 16.6 %copy-start.1 = (f32[1,16,128]{2,1,0:T(8,128)S(1)}, f32[1,16,128]{2,1,0:T(8,128)}, u32[]{:S(2)}) copy-start(f32[1,16,128]{2,1,0:T(8,128)} %param.11) | copy-start | bytes 24580
  1.7 27.0 %copy-start.3 = (s32[1,1,64]{2,1,0:T(1,128)S(1)}, s32[1,1,64]{2,1,0:T(1,128)}, u32[]{:S(2)}) copy-start(s32[1,1,64]{2,1,0:T(1,128)} %param.15) | copy-start | bytes 772
  1.7 27.3 %copy-start.2 = (s32[1,1,64]{2,1,0:T(1,128)S(1)}, s32[1,1,64]{2,1,0:T(1,128)}, u32[]{:S(2)}) copy-start(s32[1,1,64]{2,1,0:T(1,128)} %param.14) | copy-start | bytes 772
  1.7 10.1 %collective-permute-start.1 = (f32[16,1,45,128]{3,2,0,1:T(8,128)S(1)}, f32[16,1,45,128]{3,2,0,1:T(8,128)S(1)}, u32[]{:S(2)}, u32[]{:S(2)}) collective-permute-start(f32[16,1,45,128]{3,2,0,1:T(8,128)S(1)} %copy.29), channel_id=1, source_target_pairs={{0,1},{1,2},{2,3},{3,4},{4,5},{5,6},{6,7},{7,8},{8,9},{9,10},{10,1... | collective-permute-start | bytes 1105928 | tf_op jit(solution)/shard_map/ppermute | solution.py:13
  6.3 9.1 %collective-permute-start = (f32[16,1,45,128]{3,2,0,1:T(8,128)S(1)}, f32[16,1,45,128]{3,2,0,1:T(8,128)S(1)}, u32[]{:S(2)}, u32[]{:S(2)}) collective-permute-start(f32[16,1,45,128]{3,2,0,1:T(8,128)S(1)} %copy.29), channel_id=1, source_target_pairs={{1,0},{2,1},{3,2},{4,3},{5,4},{6,5},{7,6},{8,7},{9,8},{10,9},{11,1... | collective-permute-start | bytes 1105928 | tf_op jit(solution)/shard_map/ppermute | solution.py:14
  16.5 28.1 %copy-start.4 = (s32[1,1,64]{2,1,0:T(1,128)S(1)}, s32[1,1,64]{2,1,0:T(1,128)}, u32[]{:S(2)}) copy-start(s32[1,1,64]{2,1,0:T(1,128)} %param.16) | copy-start | bytes 772
  18.1 21.7 %all-to-all-start = ((f32[8,16,896]{2,1,0:T(8,128)}), f32[8,16,896]{2,1,0:T(8,128)S(1)}, u32[]{:S(2)}, u32[]{:S(2)}) async-start(f32[8,16,896]{2,1,0:T(8,128)} %pad_maximum_fusion), calls=%async_computation | async-start | bytes 917504 | tf_op jit(solution)/shard_map/all_to_all | solution.py:46
  40.9 15.0 %all-to-all-start.1 = ((f32[8,16,768]{2,1,0:T(8,128)}), f32[8,16,768]{2,1,0:T(8,128)S(1)}, u32[]{:S(2)}, u32[]{:S(2)}) async-start(f32[8,16,768]{2,1,0:T(8,128)} %bitcast.6), calls=%async_computation.1 | async-start | bytes 786432 | tf_op jit(solution)/shard_map/all_to_all | solution.py:50
  62.9 91.0 %all-to-all-start.2 = ((f32[46,128,128]{2,0,1:T(8,128)}), f32[46,128,128]{2,0,1:T(8,128)S(1)}, u32[]{:S(2)}, u32[]{:S(2)}) async-start(f32[46,128,128]{2,0,1:T(8,128)} %copy.34), calls=%async_computation.2 | async-start | bytes 6291456 | tf_op jit(solution)/shard_map/all_to_all | solution.py:72

commit v5 on v4

--- a/solution.py
+++ b/solution.py
@@ -34,12 +34,22 @@
 
     low, high = with_halo(flux, "blk", 1)
     residual = 0.25 * high - 0.75 * low + 0.5 * flux
-    padded_q = -(-components // n_pitch) * n_pitch
-    chunk_q = padded_q // n_pitch
+    chunk_q = -(-components // (2 * n_pitch))
+    split_q = chunk_q * n_pitch
     width = chunk_q * span_cells
     res = residual.reshape(pitch_local, components, span_cells)
-    res = jnp.pad(res, ((0, 0), (0, padded_q - components), (0, 0)))
-    spanned = jnp.einsum("pqs,ts->pqt", res, span_inverse[0], precision=highest)
+
+    rest = res[:, split_q:].reshape(pitch_local, (components - split_q) * span_cells)
+    rest_all = lax.all_gather(rest, "pitch", axis=0, tiled=True)
+    rest_mixed = jnp.dot(pitch_inverse[0], rest_all, precision=highest)
+    rest_smoothed = jnp.einsum(
+        "pqs,ts->pqt",
+        rest_mixed.reshape(pitch_local, components - split_q, span_cells),
+        span_inverse[0],
+        precision=highest,
+    )
+
+    spanned = jnp.einsum("pqs,ts->pqt", res[:, :split_q], span_inverse[0], precision=highest)
     chunks = spanned.reshape(pitch_local, n_pitch, width).transpose(1, 0, 2)
     pinv_rows = jnp.broadcast_to(pitch_inverse[0][None], (n_pitch,) + pitch_inverse.shape[1:])
     chunks = jnp.concatenate([chunks, pinv_rows], axis=2)
@@ -48,11 +58,12 @@
     pinv_full = gathered[:, width:]
     mixed = jnp.dot(pinv_full, gathered[:, :width], precision=highest)
     back = lax.all_to_all(mixed.reshape(n_pitch, pitch_local, width), "pitch", 0, 0, tiled=True)
-    smoothed = (
+    head_smoothed = (
         back.reshape(n_pitch, pitch_local, chunk_q, span_cells)
         .transpose(1, 0, 2, 3)
-        .reshape(pitch_local, padded_q, span_cells)[:, :components]
+        .reshape(pitch_local, split_q, span_cells)
     )
+    smoothed = jnp.concatenate([head_smoothed, rest_smoothed], axis=1)
 
     rows = smoothed.reshape(pitch_local * axial_local, components * span_cells)
     my_owner = send_owner[0, 0]

time: 162 us -> 181 us (1.12)
  between operations: 1.51 us -> 14.9 us
  waiting for transfers between devices: 96.8 us -> 103 us
  starting transfers between devices: 41.1 us -> 38 us
  matrix products: 9.75 us -> 11.9 us
    all_gather x0 -> x1, waiting for transfers between devices: none -> 9.55 us  [local(): rest_all = lax.all_gather(rest, 'pitch', axis=0, tiled=True)]
    all_to_all x1, starting transfers between devices: 17.5 us -> 14.5 us  [local(): arrived = lax.all_to_all(outgoing, 'blk', 1, 1, tiled=True)]
    dot_general x1 -> x3, matrix products: 0.48 us -> 2.82 us  [the longest x1 2.17 us: local(): rest_mixed = jnp.dot(pitch_inverse[0], rest_all, precision=highest)]
    all_to_all x1, waiting for transfers between devices: 11.2 us -> 8.98 us  [local(): lax.all_to_all(mixed.reshape(n_pitch, pitch_local, width), 'pitch', 0, 0,...]
    unnamed x12 -> x13, local copies, waits for them, and re-layouts: 3.19 us -> 3.86 us
  transfers between devices with their start and end apart: 5 -> 6, of which waited for: 4 -> 5; matrix products, arithmetic and copies ran while one was open for 2% -> 3% of each run, Pallas kernels for 0% -> 0%
where the time goes in v5:
time: 181 us
  waiting for transfers between devices  103 us (57%)
  starting transfers between devices  38 us (21%)
  between operations  14.9 us (8%)
  matrix products  11.9 us (7%)
  local copies, waits for them, and re-layouts  7.54 us (4%)
  other arithmetic  5.72 us (3%)
    all_to_all x1, waiting for transfers between devices, local(): arrived = lax.all_to_all(outgoing, 'blk', 1, 1, tiled=True)  71.4 us
    all_to_all x1, starting transfers between devices, local(): arrived = lax.all_to_all(outgoing, 'blk', 1, 1, tiled=True)  14.5 us
    all_to_all x1, starting transfers between devices, local(): gathered = lax.all_to_all(chunks, 'pitch', 0, 0, tiled=True)  10 us
    all_gather x1, waiting for transfers between devices, local(): rest_all = lax.all_gather(rest, 'pitch', axis=0, tiled=True)  9.55 us
    all_to_all x1, waiting for transfers between devices, local(): gathered = lax.all_to_all(chunks, 'pitch', 0, 0, tiled=True)  9.16 us
    all_to_all x1, waiting for transfers between devices, local(): lax.all_to_all(mixed.reshape(n_pitch, pitch_local, width), 'pitch', 0, 0,...  8.98 us
    dot_general x1, matrix products, local(): jnp.einsum('si,qit->qst', select_in.astype(jnp.float32), arrived[:compone...  5.5 us
    ppermute x1, starting transfers between devices, with_halo(): high = lax.ppermute(block, axis, backward)  5.48 us
  transfers between devices with their start and end apart: 6, of which 5 were waited for; matrix products, arithmetic and copies ran while one was open for 3% of the time, Pallas kernels for 0%

profile of v5, /device:TPU:1, one launch (start us, length us, event | category | flops | bytes accessed | tf_op | source)
XLA Modules:
  0.0 180.7 jit_solution(1025001846531597072)
XLA Ops:
  7.2 0.0 all-gather.2.cloned.1.call-start
  7.3 1.0 copy.31
  8.3 4.6 %collective-permute-start.1 = (f32[16,1,45,128]{3,2,0,1:T(8,128)S(1)}, f32[16,1,45,128]{3,2,0,1:T(8,128)S(1)}, u32[]{:S(2)}, u32[]{:S(2)}) collective-permute-start(f32[16,1,45,128]{3,2,0,1:T(8,128)S(1)} %copy.31), channel_id=1, source_target_pairs={{0,1},{1,2},{2,3},{3,4},{4,5},{5,6},{6,7},{7,8},{8,9},{9,10},{10,1... | collective-permute-start | bytes 1105928 | tf_op jit(solution)/shard_map/ppermute | solution.py:13
  12.9 5.5 %collective-permute-start = (f32[16,1,45,128]{3,2,0,1:T(8,128)S(1)}, f32[16,1,45,128]{3,2,0,1:T(8,128)S(1)}, u32[]{:S(2)}, u32[]{:S(2)}) collective-permute-start(f32[16,1,45,128]{3,2,0,1:T(8,128)S(1)} %copy.31), channel_id=1, source_target_pairs={{1,0},{2,1},{3,2},{4,3},{5,4},{6,5},{7,6},{8,7},{9,8},{10,9},{11,1... | collective-permute-start | bytes 1105928 | tf_op jit(solution)/shard_map/ppermute | solution.py:14
  18.4 3.6 %collective-permute-done = f32[16,1,45,128]{3,2,0,1:T(8,128)S(1)} collective-permute-done((f32[16,1,45,128]{3,2,0,1:T(8,128)S(1)}, f32[16,1,45,128]{3,2,0,1:T(8,128)S(1)}, u32[]{:S(2)}, u32[]{:S(2)}) %collective-permute-start) | collective-permute-done | bytes 368672 | tf_op jit(solution)/shard_map/ppermute | solution.py:14
  22.0 1.1 add_bitcast_fusion
  23.1 0.7 copy.57
  24.5 0.2 convert_reduce_fusion
  24.7 0.3 fusion.9
  25.1 0.7 pad_maximum_fusion.1
  25.9 10.0 %all-to-all-start = ((f32[8,16,512]{2,1,0:T(8,128)}), f32[8,16,512]{2,1,0:T(8,128)S(1)}, u32[]{:S(2)}, u32[]{:S(2)}) async-start(f32[8,16,512]{2,1,0:T(8,128)} %pad_maximum_fusion.1), calls=%async_computation | async-start | bytes 524288 | tf_op jit(solution)/shard_map/all_to_all | solution.py:56
  35.9 0.1 iota_compare_fusion.2
  36.0 0.1 iota_compare_fusion.1
  36.1 9.2 %all-to-all-done = f32[8,16,512]{2,1,0:T(8,128)S(1)} async-done(((f32[8,16,512]{2,1,0:T(8,128)}), f32[8,16,512]{2,1,0:T(8,128)S(1)}, u32[]{:S(2)}, u32[]{:S(2)}) %all-to-all-start) | async-done | bytes 262176 | tf_op jit(solution)/shard_map/all_to_all | solution.py:56
  45.2 1.0 fusion.7
  46.2 3.4 %all-to-all-start.1 = ((f32[8,16,384]{2,1,0:T(8,128)}), f32[8,16,384]{2,1,0:T(8,128)S(1)}, u32[]{:S(2)}, u32[]{:S(2)}) async-start(f32[8,16,384]{2,1,0:T(8,128)} %bitcast.6), calls=%async_computation.1 | async-start | bytes 393216 | tf_op jit(solution)/shard_map/all_to_all | solution.py:60
  49.6 0.2 and_reduce_fusion
  49.8 0.1 select_reduce_fusion
  49.9 9.0 %all-to-all-done.1 = f32[8,16,384]{2,1,0:T(8,128)S(1)} async-done(((f32[8,16,384]{2,1,0:T(8,128)}), f32[8,16,384]{2,1,0:T(8,128)S(1)}, u32[]{:S(2)}, u32[]{:S(2)}) %all-to-all-start.1) | async-done | bytes 196640 | tf_op jit(solution)/shard_map/all_to_all | solution.py:60
  58.9 0.1 reshape.154
  59.0 9.6 %all-gather.2.cloned.1.call-done = f32[128,2688]{1,0:T(8,128)} async-done(((f32[16,2688]{1,0:T(8,128)}), f32[128,2688]{1,0:T(8,128)}) %all-gather.2.cloned.1.call-update) | async-done | bytes 1376272 | tf_op jit(solution)/shard_map/all_gather | solution.py:43
  68.6 2.2 %convolution_bitcast_fusion.1 = f32[2,21,8,128]{3,2,1,0:T(8,128)S(1)} fusion(f32[128,2688]{1,0:T(8,128)} %all-gather.2.cloned.1.call-done, f32[1,16,128]{2,1,0:T(8,128)S(1)} %copy-done.1), kind=kOutput, calls=%fused_computation.5 | convolution fusion | flops 66060288 | bytes 1556480 | tf_op jit(solution)/shard_map/dot_general | solution.py:44
  70.8 0.3 fusion.11
  71.1 0.8 fusion.5
  72.0 2.6 %convolution_bitcast_fusion = f32[46,128,128]{2,1,0:T(8,128)S(1)} fusion(f32[46,17,128]{2,1,0:T(8,128)S(1)} %scatter.4, f32[128,1]{0,1:T(1,128)S(1)} %convert_bitcast_fusion, f32[128,16]{0,1:T(8,128)S(1)} %convert_element_type.40), kind=kOutput, calls=%fused_computation.4 | convolution fusion | flops 153749632 | bytes 3423744 | tf_op jit(solution)/shard_map/qpt,sp->sqt/dot_general | solution.py:82
  74.5 3.4 %copy.37 = f32[46,128,128]{2,0,1:T(8,128)} copy(f32[46,128,128]{2,1,0:T(8,128)S(1)} %convolution_bitcast_fusion) | data formatting | bytes 6029312 | tf_op jit(solution)/shard_map/transpose | solution.py:82
  77.9 14.5 %all-to-all-start.2 = ((f32[46,128,128]{2,0,1:T(8,128)}), f32[46,128,128]{2,0,1:T(8,128)S(1)}, u32[]{:S(2)}, u32[]{:S(2)}) async-start(f32[46,128,128]{2,0,1:T(8,128)} %copy.37), calls=%async_computation.2 | async-start | bytes 6291456 | tf_op jit(solution)/shard_map/all_to_all | solution.py:83
  92.4 2.1 %copy.39 = f32[16,1,45,128]{3,1,2,0:T(1,128)} copy(f32[16,1,45,128]{3,0,2,1:T(8,128)} %get-tuple-element.21) | data formatting | bytes 737280
  94.5 71.4 %all-to-all-done.2 = f32[46,128,128]{2,0,1:T(8,128)S(1)} async-done(((f32[46,128,128]{2,0,1:T(8,128)}), f32[46,128,128]{2,0,1:T(8,128)S(1)}, u32[]{:S(2)}, u32[]{:S(2)}) %all-to-all-start.2) | async-done | bytes 3014688 | tf_op jit(solution)/shard_map/all_to_all | solution.py:83
  165.9 2.4 %fusion.14 = s32[128]{0:T(128)S(1)} fusion(f32[46,128,128]{2,0,1:T(8,128)S(1)} %all-to-all-done.2), kind=kLoop, calls=%fused_computation.22 | loop fusion | flops 128 | bytes 1024 | tf_op jit(solution)/shard_map/convert_element_type | solution.py:85
  168.3 0.1 fusion.19
  168.4 5.5 %fusion.2 = f32[1,1,128,45,128]{4,2,3,1,0:T(8,128)} fusion(f32[45,128,128]{2,0,1:T(8,128)S(1)} %bitcast.57, bf16[1,1,128,45,128]{4,2,3,1,0:T(8,128)(2,1)} %param.13, pred[128]{0:T(512)(128)(4,1)S(1)} %fusion.19, s32[128]{0:T(128)S(1)} %fusion.14), kind=kOutput, calls=%fused_computation.3 | convolution fusion | flops 1133953024 | bytes 7373440 | tf_op jit(solution)/shard_map/si,qit->qst/dot_general | solution.py:88
  (24 shorter events, 0.3 us)
Async XLA Ops:
  7.2 17.5 %copy-start = (f32[1,128,128]{2,1,0:T(8,128)S(1)}, f32[1,128,128]{2,1,0:T(8,128)}, u32[]{:S(2)}) copy-start(f32[1,128,128]{2,1,0:T(8,128)} %param.12) | copy-start | bytes 196612
  7.2 17.3 %copy-start.3 = (s32[1,1,64]{2,1,0:T(1,128)S(1)}, s32[1,1,64]{2,1,0:T(1,128)}, u32[]{:S(2)}) copy-start(s32[1,1,64]{2,1,0:T(1,128)} %param.15) | copy-start | bytes 772
  7.2 17.9 %copy-start.1 = (f32[1,16,128]{2,1,0:T(8,128)S(1)}, f32[1,16,128]{2,1,0:T(8,128)}, u32[]{:S(2)}) copy-start(f32[1,16,128]{2,1,0:T(8,128)} %param.11) | copy-start | bytes 24580
  7.2 28.7 %copy-start.4 = (s32[1,1,64]{2,1,0:T(1,128)S(1)}, s32[1,1,64]{2,1,0:T(1,128)}, u32[]{:S(2)}) copy-start(s32[1,1,64]{2,1,0:T(1,128)} %param.16) | copy-start | bytes 772
  7.2 28.8 %copy-start.2 = (s32[1,1,64]{2,1,0:T(1,128)S(1)}, s32[1,1,64]{2,1,0:T(1,128)}, u32[]{:S(2)}) copy-start(s32[1,1,64]{2,1,0:T(1,128)} %param.14) | copy-start | bytes 772
  7.2 61.4 %all-gather.2.cloned.1.call-start = ((), (), s32[]{:S(2)}) async-start(), calls=%async_computation.3 | async-start | bytes 1548288 | tf_op jit(solution)/shard_map/all_gather | solution.py:43
  8.3 10.1 %collective-permute-start.1 = (f32[16,1,45,128]{3,2,0,1:T(8,128)S(1)}, f32[16,1,45,128]{3,2,0,1:T(8,128)S(1)}, u32[]{:S(2)}, u32[]{:S(2)}) collective-permute-start(f32[16,1,45,128]{3,2,0,1:T(8,128)S(1)} %copy.31), channel_id=1, source_target_pairs={{0,1},{1,2},{2,3},{3,4},{4,5},{5,6},{6,7},{7,8},{8,9},{9,10},{10,1... | collective-permute-start | bytes 1105928 | tf_op jit(solution)/shard_map/ppermute | solution.py:13
  12.9 9.1 %collective-permute-start = (f32[16,1,45,128]{3,2,0,1:T(8,128)S(1)}, f32[16,1,45,128]{3,2,0,1:T(8,128)S(1)}, u32[]{:S(2)}, u32[]{:S(2)}) collective-permute-start(f32[16,1,45,128]{3,2,0,1:T(8,128)S(1)} %copy.31), channel_id=1, source_target_pairs={{1,0},{2,1},{3,2},{4,3},{5,4},{6,5},{7,6},{8,7},{9,8},{10,9},{11,1... | collective-permute-start | bytes 1105928 | tf_op jit(solution)/shard_map/ppermute | solution.py:14
  25.9 19.4 %all-to-all-start = ((f32[8,16,512]{2,1,0:T(8,128)}), f32[8,16,512]{2,1,0:T(8,128)S(1)}, u32[]{:S(2)}, u32[]{:S(2)}) async-start(f32[8,16,512]{2,1,0:T(8,128)} %pad_maximum_fusion.1), calls=%async_computation | async-start | bytes 524288 | tf_op jit(solution)/shard_map/all_to_all | solution.py:56
  46.2 12.7 %all-to-all-start.1 = ((f32[8,16,384]{2,1,0:T(8,128)}), f32[8,16,384]{2,1,0:T(8,128)S(1)}, u32[]{:S(2)}, u32[]{:S(2)}) async-start(f32[8,16,384]{2,1,0:T(8,128)} %bitcast.6), calls=%async_computation.1 | async-start | bytes 393216 | tf_op jit(solution)/shard_map/all_to_all | solution.py:60
  77.9 88.0 %all-to-all-start.2 = ((f32[46,128,128]{2,0,1:T(8,128)}), f32[46,128,128]{2,0,1:T(8,128)S(1)}, u32[]{:S(2)}, u32[]{:S(2)}) async-start(f32[46,128,128]{2,0,1:T(8,128)} %copy.37), calls=%async_computation.2 | async-start | bytes 6291456 | tf_op jit(solution)/shard_map/all_to_all | solution.py:83
Sparse Core Ops, SparseCore 0:
  23.9 44.6 all-gather.1

commit v6 on v4

--- a/solution.py
+++ b/solution.py
@@ -71,11 +71,11 @@
     outgoing = jnp.einsum("qpt,sp->sqt", rows_ext, select_ext, precision=highest).transpose(1, 0, 2)
     arrived = lax.all_to_all(outgoing, "blk", 1, 1, tiled=True)
 
-    arrived_slot = arrived[components, :, 0].astype(jnp.int32)
-    select_in = arrived_slot[None, :] == jnp.arange(slot_total, dtype=jnp.int32)[:, None]
-    filled = jnp.any(select_in, axis=1)
+    slot_lanes = jnp.arange(slot_total, dtype=jnp.float32)[None, :]
+    select_in = arrived[components] == slot_lanes
+    filled = jnp.any(select_in, axis=0)
     incoming = jnp.einsum(
-        "si,qit->qst", select_in.astype(jnp.float32), arrived[:components], precision=highest
+        "is,qit->qst", select_in.astype(jnp.float32), arrived[:components], precision=highest
     )
     old_t = store_old[0, 0].transpose(1, 0, 2).astype(jnp.float32)
     storage = jnp.where(filled[None, :, None], incoming, old_t).transpose(1, 0, 2)

time: 162 us -> 160 us (0.988)
  other arithmetic: 5 us -> 2.57 us
    convert_element_type x1 -> x0, other arithmetic: 2.35 us -> none  [local(): arrived_slot = arrived[components, :, 0].astype(jnp.int32)]
where the time goes in v6:
time: 160 us; the launch traced here: 159 us
  waiting for transfers between devices  96.8 us (60%)
  starting transfers between devices  41.1 us (26%)
  matrix products  9.73 us (6%)
  local copies, waits for them, and re-layouts  7.86 us (5%)
  other arithmetic  2.57 us (2%)
    all_to_all x1, waiting for transfers between devices, local(): arrived = lax.all_to_all(outgoing, 'blk', 1, 1, tiled=True)  71.4 us
    all_to_all x1, starting transfers between devices, local(): arrived = lax.all_to_all(outgoing, 'blk', 1, 1, tiled=True)  17.5 us
    all_to_all x1, waiting for transfers between devices, local(): lax.all_to_all(mixed.reshape(n_pitch, pitch_local, width), 'pitch', 0, 0,...  11.2 us
    all_to_all x1, waiting for transfers between devices, local(): gathered = lax.all_to_all(chunks, 'pitch', 0, 0, tiled=True)  10.6 us
    all_to_all x1, starting transfers between devices, local(): gathered = lax.all_to_all(chunks, 'pitch', 0, 0, tiled=True)  10 us
    ppermute x1, starting transfers between devices, with_halo(): high = lax.ppermute(block, axis, backward)  5.48 us
    dot_general x1, matrix products, local(): jnp.einsum('is,qit->qst', select_in.astype(jnp.float32), arrived[:compone...  5.47 us
    ppermute x1, starting transfers between devices, with_halo(): low = lax.ppermute(block, axis, forward)  4.58 us
  transfers between devices with their start and end apart: 5, of which 4 were waited for; matrix products, arithmetic and copies ran while one was open for 2% of the time, Pallas kernels for 0%

profile of v6, /device:TPU:1, one launch (start us, length us, event | category | flops | bytes accessed | tf_op | source)
XLA Modules:
  0.0 159.5 jit_solution(7980012982132287988)
XLA Ops:
  0.6 0.0 copy-start
  0.7 1.0 copy.32
  1.7 0.0 copy-start.3
  1.7 4.6 %collective-permute-start.1 = (f32[16,1,45,128]{3,2,0,1:T(8,128)S(1)}, f32[16,1,45,128]{3,2,0,1:T(8,128)S(1)}, u32[]{:S(2)}, u32[]{:S(2)}) collective-permute-start(f32[16,1,45,128]{3,2,0,1:T(8,128)S(1)} %copy.32), channel_id=1, source_target_pairs={{0,1},{1,2},{2,3},{3,4},{4,5},{5,6},{6,7},{7,8},{8,9},{9,10},{10,1... | collective-permute-start | bytes 1105928 | tf_op jit(solution)/shard_map/ppermute | solution.py:13
  6.3 5.5 %collective-permute-start = (f32[16,1,45,128]{3,2,0,1:T(8,128)S(1)}, f32[16,1,45,128]{3,2,0,1:T(8,128)S(1)}, u32[]{:S(2)}, u32[]{:S(2)}) collective-permute-start(f32[16,1,45,128]{3,2,0,1:T(8,128)S(1)} %copy.32), channel_id=1, source_target_pairs={{1,0},{2,1},{3,2},{4,3},{5,4},{6,5},{7,6},{8,7},{9,8},{10,9},{11,1... | collective-permute-start | bytes 1105928 | tf_op jit(solution)/shard_map/ppermute | solution.py:14
  11.8 3.6 %collective-permute-done = f32[16,1,45,128]{3,2,0,1:T(8,128)S(1)} collective-permute-done((f32[16,1,45,128]{3,2,0,1:T(8,128)S(1)}, f32[16,1,45,128]{3,2,0,1:T(8,128)S(1)}, u32[]{:S(2)}, u32[]{:S(2)}) %collective-permute-start) | collective-permute-done | bytes 368672 | tf_op jit(solution)/shard_map/ppermute | solution.py:14
  15.4 1.1 add_bitcast_fusion
  16.5 0.0 copy-start.4
  16.5 0.5 fusion.7
  17.0 0.1 reshape.139
  17.1 0.1 copy.50
  17.3 0.8 pad_maximum_fusion
  18.1 10.0 %all-to-all-start = ((f32[8,16,896]{2,1,0:T(8,128)}), f32[8,16,896]{2,1,0:T(8,128)S(1)}, u32[]{:S(2)}, u32[]{:S(2)}) async-start(f32[8,16,896]{2,1,0:T(8,128)} %pad_maximum_fusion), calls=%async_computation | async-start | bytes 917504 | tf_op jit(solution)/shard_map/all_to_all | solution.py:46
  28.8 0.2 convert_reduce_fusion
  28.9 0.1 iota_compare_fusion.2
  29.0 0.1 iota_compare_fusion.1
  29.1 10.6 %all-to-all-done = f32[8,16,896]{2,1,0:T(8,128)S(1)} async-done(((f32[8,16,896]{2,1,0:T(8,128)}), f32[8,16,896]{2,1,0:T(8,128)S(1)}, u32[]{:S(2)}, u32[]{:S(2)}) %all-to-all-start) | async-done | bytes 458784 | tf_op jit(solution)/shard_map/all_to_all | solution.py:46
  39.7 1.2 fusion.5
  40.9 3.5 %all-to-all-start.1 = ((f32[8,16,768]{2,1,0:T(8,128)}), f32[8,16,768]{2,1,0:T(8,128)S(1)}, u32[]{:S(2)}, u32[]{:S(2)}) async-start(f32[8,16,768]{2,1,0:T(8,128)} %bitcast.6), calls=%async_computation.1 | async-start | bytes 786432 | tf_op jit(solution)/shard_map/all_to_all | solution.py:50
  44.4 0.2 and_reduce_fusion
  44.6 0.1 select_reduce_fusion
  44.8 11.2 %all-to-all-done.1 = f32[8,16,768]{2,1,0:T(8,128)S(1)} async-done(((f32[8,16,768]{2,1,0:T(8,128)}), f32[8,16,768]{2,1,0:T(8,128)S(1)}, u32[]{:S(2)}, u32[]{:S(2)}) %all-to-all-start.1) | async-done | bytes 393248 | tf_op jit(solution)/shard_map/all_to_all | solution.py:50
  55.9 0.1 reshape.142
  56.0 0.1 copy.36
  56.1 0.8 slice_bitcast_fusion
  56.9 2.6 %convolution_bitcast_fusion = f32[46,128,128]{2,1,0:T(8,128)S(1)} fusion(f32[46,17,128]{2,1,0:T(8,128)S(1)} %scatter.4, f32[128,1]{0,1:T(1,128)S(1)} %convert_bitcast_fusion, f32[128,16]{0,1:T(8,128)S(1)} %convert_element_type.32), kind=kOutput, calls=%fused_computation.4 | convolution fusion | flops 153749632 | bytes 3423744 | tf_op jit(solution)/shard_map/qpt,sp->sqt/dot_general | solution.py:71
  59.5 3.4 %copy.37 = f32[46,128,128]{2,0,1:T(8,128)} copy(f32[46,128,128]{2,1,0:T(8,128)S(1)} %convolution_bitcast_fusion) | data formatting | bytes 6029312 | tf_op jit(solution)/shard_map/transpose | solution.py:71
  62.9 17.5 %all-to-all-start.2 = ((f32[46,128,128]{2,0,1:T(8,128)}), f32[46,128,128]{2,0,1:T(8,128)S(1)}, u32[]{:S(2)}, u32[]{:S(2)}) async-start(f32[46,128,128]{2,0,1:T(8,128)} %copy.37), calls=%async_computation.2 | async-start | bytes 6291456 | tf_op jit(solution)/shard_map/all_to_all | solution.py:72
  80.4 2.1 %copy.40 = f32[16,1,45,128]{3,1,2,0:T(1,128)} copy(f32[16,1,45,128]{3,0,2,1:T(8,128)} %get-tuple-element.23) | data formatting | bytes 737280
  82.5 71.4 %all-to-all-done.2 = f32[46,128,128]{2,0,1:T(8,128)S(1)} async-done(((f32[46,128,128]{2,0,1:T(8,128)}), f32[46,128,128]{2,0,1:T(8,128)S(1)}, u32[]{:S(2)}, u32[]{:S(2)}) %all-to-all-start.2) | async-done | bytes 3014688 | tf_op jit(solution)/shard_map/all_to_all | solution.py:72
  153.9 0.1 slice.45
  154.0 5.5 %fusion.2 = f32[1,1,128,45,128]{4,2,3,1,0:T(8,128)} fusion(f32[45,128,128]{2,0,1:T(8,128)S(1)} %bitcast.43, bf16[1,1,128,45,128]{4,2,3,1,0:T(8,128)(2,1)} %param.13, pred[128]{0:T(512)(128)(4,1)S(1)} %get-tuple-element.20, pred[128,128]{1,0:T(32,128)(4,1)S(1)} %get-tuple-element.21), kind=kOutput, calls=%fused_computation.3 | convolution fusion | flops 1133936640 | bytes 7389312 | tf_op jit(solution)/shard_map/is,qit->qst/dot_general | solution.py:77
  (17 shorter events, 0.2 us)
Async XLA Ops:
  0.6 15.9 %copy-start = (f32[1,128,128]{2,1,0:T(8,128)S(1)}, f32[1,128,128]{2,1,0:T(8,128)}, u32[]{:S(2)}) copy-start(f32[1,128,128]{2,1,0:T(8,128)} %param.12) | copy-start | bytes 196612
  0.6 16.6 %copy-start.1 = (f32[1,16,128]{2,1,0:T(8,128)S(1)}, f32[1,16,128]{2,1,0:T(8,128)}, u32[]{:S(2)}) copy-start(f32[1,16,128]{2,1,0:T(8,128)} %param.11) | copy-start | bytes 24580
  1.7 27.0 %copy-start.3 = (s32[1,1,64]{2,1,0:T(1,128)S(1)}, s32[1,1,64]{2,1,0:T(1,128)}, u32[]{:S(2)}) copy-start(s32[1,1,64]{2,1,0:T(1,128)} %param.15) | copy-start | bytes 772
  1.7 27.3 %copy-start.2 = (s32[1,1,64]{2,1,0:T(1,128)S(1)}, s32[1,1,64]{2,1,0:T(1,128)}, u32[]{:S(2)}) copy-start(s32[1,1,64]{2,1,0:T(1,128)} %param.14) | copy-start | bytes 772
  1.7 10.1 %collective-permute-start.1 = (f32[16,1,45,128]{3,2,0,1:T(8,128)S(1)}, f32[16,1,45,128]{3,2,0,1:T(8,128)S(1)}, u32[]{:S(2)}, u32[]{:S(2)}) collective-permute-start(f32[16,1,45,128]{3,2,0,1:T(8,128)S(1)} %copy.32), channel_id=1, source_target_pairs={{0,1},{1,2},{2,3},{3,4},{4,5},{5,6},{6,7},{7,8},{8,9},{9,10},{10,1... | collective-permute-start | bytes 1105928 | tf_op jit(solution)/shard_map/ppermute | solution.py:13
  6.3 9.1 %collective-permute-start = (f32[16,1,45,128]{3,2,0,1:T(8,128)S(1)}, f32[16,1,45,128]{3,2,0,1:T(8,128)S(1)}, u32[]{:S(2)}, u32[]{:S(2)}) collective-permute-start(f32[16,1,45,128]{3,2,0,1:T(8,128)S(1)} %copy.32), channel_id=1, source_target_pairs={{1,0},{2,1},{3,2},{4,3},{5,4},{6,5},{7,6},{8,7},{9,8},{10,9},{11,1... | collective-permute-start | bytes 1105928 | tf_op jit(solution)/shard_map/ppermute | solution.py:14
  16.5 28.1 %copy-start.4 = (s32[1,1,64]{2,1,0:T(1,128)S(1)}, s32[1,1,64]{2,1,0:T(1,128)}, u32[]{:S(2)}) copy-start(s32[1,1,64]{2,1,0:T(1,128)} %param.16) | copy-start | bytes 772
  18.1 21.7 %all-to-all-start = ((f32[8,16,896]{2,1,0:T(8,128)}), f32[8,16,896]{2,1,0:T(8,128)S(1)}, u32[]{:S(2)}, u32[]{:S(2)}) async-start(f32[8,16,896]{2,1,0:T(8,128)} %pad_maximum_fusion), calls=%async_computation | async-start | bytes 917504 | tf_op jit(solution)/shard_map/all_to_all | solution.py:46
  40.9 15.0 %all-to-all-start.1 = ((f32[8,16,768]{2,1,0:T(8,128)}), f32[8,16,768]{2,1,0:T(8,128)S(1)}, u32[]{:S(2)}, u32[]{:S(2)}) async-start(f32[8,16,768]{2,1,0:T(8,128)} %bitcast.6), calls=%async_computation.1 | async-start | bytes 786432 | tf_op jit(solution)/shard_map/all_to_all | solution.py:50
  62.9 91.0 %all-to-all-start.2 = ((f32[46,128,128]{2,0,1:T(8,128)}), f32[46,128,128]{2,0,1:T(8,128)S(1)}, u32[]{:S(2)}, u32[]{:S(2)}) async-start(f32[46,128,128]{2,0,1:T(8,128)} %copy.37), calls=%async_computation.2 | async-start | bytes 6291456 | tf_op jit(solution)/shard_map/all_to_all | solution.py:72

commit v7 on v6

--- a/solution.py
+++ b/solution.py
@@ -32,8 +32,9 @@
     entries = send_owner.shape[2]
     slot_total = store_old.shape[2]
 
-    low, high = with_halo(flux, "blk", 1)
-    residual = 0.25 * high - 0.75 * low + 0.5 * flux
+    flat = flux.reshape(pitch_local * axial_local * components, span_cells)
+    low, high = with_halo(flat, "blk", 0)
+    residual = 0.25 * high - 0.75 * low + 0.5 * flat
     padded_q = -(-components // n_pitch) * n_pitch
     chunk_q = padded_q // n_pitch
     width = chunk_q * span_cells

time: 160 us -> 159 us (level)
  no operation moved by 1% of the time
where the time goes in v7:
time: 159 us
  waiting for transfers between devices  97.6 us (61%)
  starting transfers between devices  40.3 us (25%)
  matrix products  9.74 us (6%)
  local copies, waits for them, and re-layouts  6.83 us (4%)
  other arithmetic  2.56 us (2%)
    all_to_all x1, waiting for transfers between devices, local(): arrived = lax.all_to_all(outgoing, 'blk', 1, 1, tiled=True)  71.4 us
    all_to_all x1, starting transfers between devices, local(): arrived = lax.all_to_all(outgoing, 'blk', 1, 1, tiled=True)  16.6 us
    all_to_all x1, waiting for transfers between devices, local(): lax.all_to_all(mixed.reshape(n_pitch, pitch_local, width), 'pitch', 0, 0,...  11.8 us
    all_to_all x1, waiting for transfers between devices, local(): gathered = lax.all_to_all(chunks, 'pitch', 0, 0, tiled=True)  10.8 us
    all_to_all x1, starting transfers between devices, local(): gathered = lax.all_to_all(chunks, 'pitch', 0, 0, tiled=True)  10 us
    ppermute x1, starting transfers between devices, with_halo(): high = lax.ppermute(block, axis, backward)  5.48 us
    dot_general x1, matrix products, local(): jnp.einsum('is,qit->qst', select_in.astype(jnp.float32), arrived[:compone...  5.47 us
    ppermute x1, starting transfers between devices, with_halo(): low = lax.ppermute(block, axis, forward)  4.71 us
  transfers between devices with their start and end apart: 5, of which 4 were waited for; matrix products, arithmetic and copies ran while one was open for 2% of the time, Pallas kernels for 0%

profile of v7, /device:TPU:1, one launch (start us, length us, event | category | flops | bytes accessed | tf_op | source)
XLA Modules:
  0.0 158.5 jit_solution(3885424978479661966)
XLA Ops:
  0.6 0.0 copy-start
  0.7 4.7 %collective-permute-start.1 = (f32[720,128]{1,0:T(8,128)}, f32[720,128]{1,0:T(8,128)S(1)}, u32[]{:S(2)}, u32[]{:S(2)}) collective-permute-start(f32[720,128]{1,0:T(8,128)} %bitcast.47), channel_id=1, source_target_pairs={{0,1},{1,2},{2,3},{3,4},{4,5},{5,6},{6,7},{7,8},{8,9},{9,10},{10,1... | collective-permute-start | bytes 1105928 | tf_op jit(solution)/shard_map/ppermute | solution.py:13
  5.4 5.5 %collective-permute-start = (f32[720,128]{1,0:T(8,128)}, f32[720,128]{1,0:T(8,128)S(1)}, u32[]{:S(2)}, u32[]{:S(2)}) collective-permute-start(f32[720,128]{1,0:T(8,128)} %bitcast.48), channel_id=1, source_target_pairs={{1,0},{2,1},{3,2},{4,3},{5,4},{6,5},{7,6},{8,7},{9,8},{10,9},{11,1... | collective-permute-start | bytes 1105928 | tf_op jit(solution)/shard_map/ppermute | solution.py:14
  10.9 0.0 collective-permute-done.1
  10.9 3.5 %collective-permute-done = f32[720,128]{1,0:T(8,128)S(1)} collective-permute-done((f32[720,128]{1,0:T(8,128)}, f32[720,128]{1,0:T(8,128)S(1)}, u32[]{:S(2)}, u32[]{:S(2)}) %collective-permute-start) | collective-permute-done | bytes 368672 | tf_op jit(solution)/shard_map/ppermute | solution.py:14
  14.4 1.1 multiply_add_fusion
  15.6 0.0 copy-start.4
  15.6 0.5 fusion.7
  16.1 0.1 reshape.143
  16.1 0.1 copy.37
  16.3 0.8 pad_maximum_fusion
  17.1 10.0 %all-to-all-start = ((f32[8,16,896]{2,1,0:T(8,128)}), f32[8,16,896]{2,1,0:T(8,128)S(1)}, u32[]{:S(2)}, u32[]{:S(2)}) async-start(f32[8,16,896]{2,1,0:T(8,128)} %pad_maximum_fusion), calls=%async_computation | async-start | bytes 917504 | tf_op jit(solution)/shard_map/all_to_all | solution.py:47
  27.8 0.2 convert_reduce_fusion
  28.0 0.1 iota_compare_fusion.2
  28.1 0.0 copy-done.2
  28.1 0.1 iota_compare_fusion.1
  28.2 10.8 %all-to-all-done = f32[8,16,896]{2,1,0:T(8,128)S(1)} async-done(((f32[8,16,896]{2,1,0:T(8,128)}), f32[8,16,896]{2,1,0:T(8,128)S(1)}, u32[]{:S(2)}, u32[]{:S(2)}) %all-to-all-start) | async-done | bytes 458784 | tf_op jit(solution)/shard_map/all_to_all | solution.py:47
  39.0 1.2 fusion.5
  40.2 3.5 %all-to-all-start.1 = ((f32[8,16,768]{2,1,0:T(8,128)}), f32[8,16,768]{2,1,0:T(8,128)S(1)}, u32[]{:S(2)}, u32[]{:S(2)}) async-start(f32[8,16,768]{2,1,0:T(8,128)} %bitcast.6), calls=%async_computation.1 | async-start | bytes 786432 | tf_op jit(solution)/shard_map/all_to_all | solution.py:51
  43.7 0.2 and_reduce_fusion
  43.9 0.1 select_reduce_fusion
  44.0 11.8 %all-to-all-done.1 = f32[8,16,768]{2,1,0:T(8,128)S(1)} async-done(((f32[8,16,768]{2,1,0:T(8,128)}), f32[8,16,768]{2,1,0:T(8,128)S(1)}, u32[]{:S(2)}, u32[]{:S(2)}) %all-to-all-start.1) | async-done | bytes 393248 | tf_op jit(solution)/shard_map/all_to_all | solution.py:51
  55.9 0.1 reshape.146
  55.9 0.1 copy.24
  56.0 0.8 slice_bitcast_fusion
  56.9 2.6 %convolution_bitcast_fusion = f32[46,128,128]{2,1,0:T(8,128)S(1)} fusion(f32[46,17,128]{2,1,0:T(8,128)S(1)} %scatter.4, f32[128,1]{0,1:T(1,128)S(1)} %convert_bitcast_fusion, f32[128,16]{0,1:T(8,128)S(1)} %convert_element_type.32), kind=kOutput, calls=%fused_computation.4 | convolution fusion | flops 153749632 | bytes 3423744 | tf_op jit(solution)/shard_map/qpt,sp->sqt/dot_general | solution.py:72
  59.5 3.4 %copy.25 = f32[46,128,128]{2,0,1:T(8,128)} copy(f32[46,128,128]{2,1,0:T(8,128)S(1)} %convolution_bitcast_fusion) | data formatting | bytes 6029312 | tf_op jit(solution)/shard_map/transpose | solution.py:72
  62.9 16.6 %all-to-all-start.2 = ((f32[46,128,128]{2,0,1:T(8,128)}), f32[46,128,128]{2,0,1:T(8,128)S(1)}, u32[]{:S(2)}, u32[]{:S(2)}) async-start(f32[46,128,128]{2,0,1:T(8,128)} %copy.25), calls=%async_computation.2 | async-start | bytes 6291456 | tf_op jit(solution)/shard_map/all_to_all | solution.py:73
  79.5 2.1 %copy.28 = f32[16,1,45,128]{3,1,2,0:T(1,128)} copy(f32[16,1,45,128]{3,0,2,1:T(8,128)} %get-tuple-element.23) | data formatting | bytes 737280
  81.6 71.4 %all-to-all-done.2 = f32[46,128,128]{2,0,1:T(8,128)S(1)} async-done(((f32[46,128,128]{2,0,1:T(8,128)}), f32[46,128,128]{2,0,1:T(8,128)S(1)}, u32[]{:S(2)}, u32[]{:S(2)}) %all-to-all-start.2) | async-done | bytes 3014688 | tf_op jit(solution)/shard_map/all_to_all | solution.py:73
  152.9 0.1 slice.45
  153.0 5.5 %fusion.2 = f32[1,1,128,45,128]{4,2,3,1,0:T(8,128)} fusion(f32[45,128,128]{2,0,1:T(8,128)S(1)} %bitcast.42, bf16[1,1,128,45,128]{4,2,3,1,0:T(8,128)(2,1)} %param.13, pred[128]{0:T(512)(128)(4,1)S(1)} %get-tuple-element.20, pred[128,128]{1,0:T(32,128)(4,1)S(1)} %get-tuple-element.21), kind=kOutput, calls=%fused_computation.3 | convolution fusion | flops 1133936640 | bytes 7389312 | tf_op jit(solution)/shard_map/is,qit->qst/dot_general | solution.py:78
  (17 shorter events, 0.2 us)
Async XLA Ops:
  0.6 14.9 %copy-start = (f32[1,128,128]{2,1,0:T(8,128)S(1)}, f32[1,128,128]{2,1,0:T(8,128)}, u32[]{:S(2)}) copy-start(f32[1,128,128]{2,1,0:T(8,128)} %param.12) | copy-start | bytes 196612
  0.6 15.6 %copy-start.1 = (f32[1,16,128]{2,1,0:T(8,128)S(1)}, f32[1,16,128]{2,1,0:T(8,128)}, u32[]{:S(2)}) copy-start(f32[1,16,128]{2,1,0:T(8,128)} %param.11) | copy-start | bytes 24580
  0.7 27.1 %copy-start.3 = (s32[1,1,64]{2,1,0:T(1,128)S(1)}, s32[1,1,64]{2,1,0:T(1,128)}, u32[]{:S(2)}) copy-start(s32[1,1,64]{2,1,0:T(1,128)} %param.15) | copy-start | bytes 772
  0.7 27.4 %copy-start.2 = (s32[1,1,64]{2,1,0:T(1,128)S(1)}, s32[1,1,64]{2,1,0:T(1,128)}, u32[]{:S(2)}) copy-start(s32[1,1,64]{2,1,0:T(1,128)} %param.14) | copy-start | bytes 772
  0.7 10.2 %collective-permute-start.1 = (f32[720,128]{1,0:T(8,128)}, f32[720,128]{1,0:T(8,128)S(1)}, u32[]{:S(2)}, u32[]{:S(2)}) collective-permute-start(f32[720,128]{1,0:T(8,128)} %bitcast.47), channel_id=1, source_target_pairs={{0,1},{1,2},{2,3},{3,4},{4,5},{5,6},{6,7},{7,8},{8,9},{9,10},{10,1... | collective-permute-start | bytes 1105928 | tf_op jit(solution)/shard_map/ppermute | solution.py:13
  5.4 9.0 %collective-permute-start = (f32[720,128]{1,0:T(8,128)}, f32[720,128]{1,0:T(8,128)S(1)}, u32[]{:S(2)}, u32[]{:S(2)}) collective-permute-start(f32[720,128]{1,0:T(8,128)} %bitcast.48), channel_id=1, source_target_pairs={{1,0},{2,1},{3,2},{4,3},{5,4},{6,5},{7,6},{8,7},{9,8},{10,9},{11,1... | collective-permute-start | bytes 1105928 | tf_op jit(solution)/shard_map/ppermute | solution.py:14
  15.6 28.3 %copy-start.4 = (s32[1,1,64]{2,1,0:T(1,128)S(1)}, s32[1,1,64]{2,1,0:T(1,128)}, u32[]{:S(2)}) copy-start(s32[1,1,64]{2,1,0:T(1,128)} %param.16) | copy-start | bytes 772
  17.1 21.9 %all-to-all-start = ((f32[8,16,896]{2,1,0:T(8,128)}), f32[8,16,896]{2,1,0:T(8,128)S(1)}, u32[]{:S(2)}, u32[]{:S(2)}) async-start(f32[8,16,896]{2,1,0:T(8,128)} %pad_maximum_fusion), calls=%async_computation | async-start | bytes 917504 | tf_op jit(solution)/shard_map/all_to_all | solution.py:47
  40.2 15.6 %all-to-all-start.1 = ((f32[8,16,768]{2,1,0:T(8,128)}), f32[8,16,768]{2,1,0:T(8,128)S(1)}, u32[]{:S(2)}, u32[]{:S(2)}) async-start(f32[8,16,768]{2,1,0:T(8,128)} %bitcast.6), calls=%async_computation.1 | async-start | bytes 786432 | tf_op jit(solution)/shard_map/all_to_all | solution.py:51
  62.9 90.1 %all-to-all-start.2 = ((f32[46,128,128]{2,0,1:T(8,128)}), f32[46,128,128]{2,0,1:T(8,128)S(1)}, u32[]{:S(2)}, u32[]{:S(2)}) async-start(f32[46,128,128]{2,0,1:T(8,128)} %copy.25), calls=%async_computation.2 | async-start | bytes 6291456 | tf_op jit(solution)/shard_map/all_to_all | solution.py:73

commit v8 on v7

--- a/solution.py
+++ b/solution.py
@@ -13,6 +13,21 @@
     low = lax.ppermute(block, axis, forward)
     high = lax.ppermute(block, axis, backward)
     return low, high
+
+
+def exact_select(spec, select, values):
+    hi_f = lax.reduce_precision(values, exponent_bits=8, mantissa_bits=7)
+    rest = values - hi_f
+    mid_f = lax.reduce_precision(rest, exponent_bits=8, mantissa_bits=7)
+    lo_f = lax.reduce_precision(rest - mid_f, exponent_bits=8, mantissa_bits=7)
+    select = select.astype(jnp.bfloat16)
+    total = None
+    for part in (hi_f, mid_f, lo_f):
+        term = jnp.einsum(
+            spec, select, part.astype(jnp.bfloat16), preferred_element_type=jnp.float32
+        )
+        total = term if total is None else total + term
+    return total
 
 
 def entry_ranks(owner):
@@ -69,15 +84,14 @@
     rows_ext = jnp.pad(smoothed.transpose(1, 0, 2), ((0, 1), (0, 1), (0, 0)))
     rows_ext = rows_ext.at[components, pitch_local * axial_local].set(1.0)
     select_ext = jnp.concatenate([select_out, tag.astype(jnp.float32)[:, None]], axis=1)
-    outgoing = jnp.einsum("qpt,sp->sqt", rows_ext, select_ext, precision=highest).transpose(1, 0, 2)
+    outgoing = exact_select("sp,qpt->qst", select_ext, rows_ext)
     arrived = lax.all_to_all(outgoing, "blk", 1, 1, tiled=True)
 
     slot_lanes = jnp.arange(slot_total, dtype=jnp.float32)[None, :]
     select_in = arrived[components] == slot_lanes
     filled = jnp.any(select_in, axis=0)
-    incoming = jnp.einsum(
-        "is,qit->qst", select_in.astype(jnp.float32), arrived[:components], precision=highest
-    )
+    incoming = exact_select("is,qit->qst", select_in, arrived[:components])
+
     old_t = store_old[0, 0].transpose(1, 0, 2).astype(jnp.float32)
     storage = jnp.where(filled[None, :, None], incoming, old_t).transpose(1, 0, 2)
     return (smoothed.reshape(flux.shape), storage[None, None])

time: 159 us -> 159 us (level)
    transpose x1 -> x0, local copies, waits for them, and re-layouts: 3.4 us -> none  [local(): jnp.einsum('qpt,sp->sqt', rows_ext, select_ext, precision=highest)]
    add x0 -> x1, local copies, waits for them, and re-layouts: none -> 2.59 us  [exact_select(): total = term if total is None else total + term]
    dot_general x2 -> x6, matrix products: 8.04 us -> 8.56 us  [exact_select(): jnp.einsum(spec, select, part.astype(jnp.bfloat16), preferred_element_typ...]
where the time goes in v8:
time: 159 us
  waiting for transfers between devices  97.6 us (61%)
  starting transfers between devices  40.3 us (25%)
  matrix products  10.3 us (6%)
  local copies, waits for them, and re-layouts  6.39 us (4%)
  other arithmetic  2.56 us (2%)
    all_to_all x1, waiting for transfers between devices, local(): arrived = lax.all_to_all(outgoing, 'blk', 1, 1, tiled=True)  71.4 us
    all_to_all x1, starting transfers between devices, local(): arrived = lax.all_to_all(outgoing, 'blk', 1, 1, tiled=True)  16.6 us
    all_to_all x1, waiting for transfers between devices, local(): lax.all_to_all(mixed.reshape(n_pitch, pitch_local, width), 'pitch', 0, 0,...  11.9 us
    all_to_all x1, waiting for transfers between devices, local(): gathered = lax.all_to_all(chunks, 'pitch', 0, 0, tiled=True)  10.8 us
    all_to_all x1, starting transfers between devices, local(): gathered = lax.all_to_all(chunks, 'pitch', 0, 0, tiled=True)  10 us
    dot_general x6, matrix products, exact_select(): jnp.einsum(spec, select, part.astype(jnp.bfloat16), preferred_element_typ...  8.56 us
    ppermute x1, starting transfers between devices, with_halo(): high = lax.ppermute(block, axis, backward)  5.48 us
    ppermute x1, starting transfers between devices, with_halo(): low = lax.ppermute(block, axis, forward)  4.71 us
  transfers between devices with their start and end apart: 5, of which 4 were waited for; matrix products, arithmetic and copies ran while one was open for 2% of the time, Pallas kernels for 0%

profile of v8, /device:TPU:1, one launch (start us, length us, event | category | flops | bytes accessed | tf_op | source)
XLA Modules:
  0.0 158.6 jit_solution(5992717683617445071)
XLA Ops:
  0.7 4.7 %collective-permute-start.1 = (f32[720,128]{1,0:T(8,128)}, f32[720,128]{1,0:T(8,128)S(1)}, u32[]{:S(2)}, u32[]{:S(2)}) collective-permute-start(f32[720,128]{1,0:T(8,128)} %bitcast.56), channel_id=1, source_target_pairs={{0,1},{1,2},{2,3},{3,4},{4,5},{5,6},{6,7},{7,8},{8,9},{9,10},{10,1... | collective-permute-start | bytes 1105928 | tf_op jit(solution)/shard_map/ppermute | solution.py:13
  5.4 5.5 %collective-permute-start = (f32[720,128]{1,0:T(8,128)}, f32[720,128]{1,0:T(8,128)S(1)}, u32[]{:S(2)}, u32[]{:S(2)}) collective-permute-start(f32[720,128]{1,0:T(8,128)} %bitcast.57), channel_id=1, source_target_pairs={{1,0},{2,1},{3,2},{4,3},{5,4},{6,5},{7,6},{8,7},{9,8},{10,9},{11,1... | collective-permute-start | bytes 1105928 | tf_op jit(solution)/shard_map/ppermute | solution.py:14
  10.9 3.5 %collective-permute-done = f32[720,128]{1,0:T(8,128)S(1)} collective-permute-done((f32[720,128]{1,0:T(8,128)}, f32[720,128]{1,0:T(8,128)S(1)}, u32[]{:S(2)}, u32[]{:S(2)}) %collective-permute-start) | collective-permute-done | bytes 368672 | tf_op jit(solution)/shard_map/ppermute | solution.py:14
  14.5 1.1 multiply_add_fusion
  15.6 0.5 fusion.10
  16.1 0.1 reshape.144
  16.1 0.1 copy.56
  16.3 0.8 pad_maximum_fusion
  17.1 10.0 %all-to-all-start = ((f32[8,16,896]{2,1,0:T(8,128)}), f32[8,16,896]{2,1,0:T(8,128)S(1)}, u32[]{:S(2)}, u32[]{:S(2)}) async-start(f32[8,16,896]{2,1,0:T(8,128)} %pad_maximum_fusion), calls=%async_computation | async-start | bytes 917504 | tf_op jit(solution)/shard_map/all_to_all | solution.py:62
  27.8 0.2 convert_reduce_fusion
  28.0 0.1 iota_compare_fusion.2
  28.1 0.1 iota_compare_fusion.1
  28.2 10.8 %all-to-all-done = f32[8,16,896]{2,1,0:T(8,128)S(1)} async-done(((f32[8,16,896]{2,1,0:T(8,128)}), f32[8,16,896]{2,1,0:T(8,128)S(1)}, u32[]{:S(2)}, u32[]{:S(2)}) %all-to-all-start) | async-done | bytes 458784 | tf_op jit(solution)/shard_map/all_to_all | solution.py:62
  39.0 1.2 fusion.8
  40.2 3.5 %all-to-all-start.1 = ((f32[8,16,768]{2,1,0:T(8,128)}), f32[8,16,768]{2,1,0:T(8,128)S(1)}, u32[]{:S(2)}, u32[]{:S(2)}) async-start(f32[8,16,768]{2,1,0:T(8,128)} %bitcast.6), calls=%async_computation.1 | async-start | bytes 786432 | tf_op jit(solution)/shard_map/all_to_all | solution.py:66
  43.7 0.1 select_reduce_fusion
  43.8 0.2 and_reduce_fusion
  44.0 11.9 %all-to-all-done.1 = f32[8,16,768]{2,1,0:T(8,128)S(1)} async-done(((f32[8,16,768]{2,1,0:T(8,128)}), f32[8,16,768]{2,1,0:T(8,128)S(1)}, u32[]{:S(2)}, u32[]{:S(2)}) %all-to-all-start.1) | async-done | bytes 393248 | tf_op jit(solution)/shard_map/all_to_all | solution.py:66
  55.9 0.1 copy.32
  56.0 0.8 slice_bitcast_fusion
  56.9 0.6 fusion.14
  57.5 0.2 copy-done.1
  57.7 0.6 fusion.13
  58.3 1.7 %add_bitcast_fusion = f32[46,128,128]{1,2,0:T(8,128)S(1)} fusion(f32[46,128,128]{2,1,0:T(8,128)S(1)} %fusion.13, f32[46,128,128]{2,1,0:T(8,128)S(1)} %fusion.14, f32[46,17,128]{2,1,0:T(8,128)} %copy-done.1, bf16[128,1]{0,1:T(2,128)(2,1)S(1)} %convert_bitcast_fusion, bf16[128,16]{0,1:T(8,128)(2,1)S(1)} %convert_convert_fusion), kind=kOutput, calls=%fused_computation.4 | convolution fusion | flops 27741184 | bytes 9448704 | tf_op jit(solution)/shard_map/sp,qpt->qst/dot_general | solution.py:26
  60.0 2.6 %copy.33 = f32[46,128,128]{2,0,1:T(8,128)} copy(f32[46,128,128]{1,2,0:T(8,128)S(1)} %add_bitcast_fusion) | data formatting | bytes 6029312 | tf_op jit(solution)/shard_map/add | solution.py:29
  62.6 16.6 %all-to-all-start.2 = ((f32[46,128,128]{2,0,1:T(8,128)}), f32[46,128,128]{2,0,1:T(8,128)S(1)}, u32[]{:S(2)}, u32[]{:S(2)}) async-start(f32[46,128,128]{2,0,1:T(8,128)} %copy.33), calls=%async_computation.2 | async-start | bytes 6291456 | tf_op jit(solution)/shard_map/all_to_all | solution.py:88
  79.2 2.1 %copy.38 = f32[16,1,45,128]{3,1,2,0:T(1,128)} copy(f32[16,1,45,128]{3,0,2,1:T(8,128)} %get-tuple-element.23) | data formatting | bytes 737280
  81.3 71.4 %all-to-all-done.2 = f32[46,128,128]{2,0,1:T(8,128)S(1)} async-done(((f32[46,128,128]{2,0,1:T(8,128)}), f32[46,128,128]{2,0,1:T(8,128)S(1)}, u32[]{:S(2)}, u32[]{:S(2)}) %all-to-all-start.2) | async-done | bytes 3014688 | tf_op jit(solution)/shard_map/all_to_all | solution.py:88
  152.8 1.2 fusion.4
  154.0 1.2 fusion.5
  155.1 0.2 copy-done.2
  155.3 3.3 %fusion.2 = f32[1,1,128,45,128]{4,2,3,1,0:T(8,128)} fusion(f32[128,45,128]{2,0,1:T(8,128)S(1)} %fusion.4, f32[128,45,128]{2,0,1:T(8,128)S(1)} %fusion.5, f32[45,128,128]{2,0,1:T(8,128)S(1)} %bitcast.51, bf16[1,1,128,45,128]{4,2,3,1,0:T(8,128)(2,1)S(1)} %copy-done.2, pred[128]{0:T(512)(128)(4,1)S(1)} %get-tuple-element.20, ...), kind=kOutput, calls=%fused_computation.8 | convolution fusion | flops 196116480 | bytes 13287552 | tf_op jit(solution)/shard_map/is,qit->qst/dot_general | solution.py:26
  (25 shorter events, 0.3 us)
Async XLA Ops:
  0.6 14.9 %copy-start = (f32[1,128,128]{2,1,0:T(8,128)S(1)}, f32[1,128,128]{2,1,0:T(8,128)}, u32[]{:S(2)}) copy-start(f32[1,128,128]{2,1,0:T(8,128)} %param.12) | copy-start | bytes 196612
  0.6 15.6 %copy-start.3 = (f32[1,16,128]{2,1,0:T(8,128)S(1)}, f32[1,16,128]{2,1,0:T(8,128)}, u32[]{:S(2)}) copy-start(f32[1,16,128]{2,1,0:T(8,128)} %param.11) | copy-start | bytes 24580
  0.7 26.5 %copy-start.6 = (s32[1,1,64]{2,1,0:T(1,128)S(1)}, s32[1,1,64]{2,1,0:T(1,128)}, u32[]{:S(2)}) copy-start(s32[1,1,64]{2,1,0:T(1,128)} %param.16) | copy-start | bytes 772
  0.7 27.1 %copy-start.5 = (s32[1,1,64]{2,1,0:T(1,128)S(1)}, s32[1,1,64]{2,1,0:T(1,128)}, u32[]{:S(2)}) copy-start(s32[1,1,64]{2,1,0:T(1,128)} %param.15) | copy-start | bytes 772
  0.7 27.4 %copy-start.4 = (s32[1,1,64]{2,1,0:T(1,128)S(1)}, s32[1,1,64]{2,1,0:T(1,128)}, u32[]{:S(2)}) copy-start(s32[1,1,64]{2,1,0:T(1,128)} %param.14) | copy-start | bytes 772
  0.7 10.2 %collective-permute-start.1 = (f32[720,128]{1,0:T(8,128)}, f32[720,128]{1,0:T(8,128)S(1)}, u32[]{:S(2)}, u32[]{:S(2)}) collective-permute-start(f32[720,128]{1,0:T(8,128)} %bitcast.56), channel_id=1, source_target_pairs={{0,1},{1,2},{2,3},{3,4},{4,5},{5,6},{6,7},{7,8},{8,9},{9,10},{10,1... | collective-permute-start | bytes 1105928 | tf_op jit(solution)/shard_map/ppermute | solution.py:13
  5.4 9.0 %collective-permute-start = (f32[720,128]{1,0:T(8,128)}, f32[720,128]{1,0:T(8,128)S(1)}, u32[]{:S(2)}, u32[]{:S(2)}) collective-permute-start(f32[720,128]{1,0:T(8,128)} %bitcast.57), channel_id=1, source_target_pairs={{1,0},{2,1},{3,2},{4,3},{5,4},{6,5},{7,6},{8,7},{9,8},{10,9},{11,1... | collective-permute-start | bytes 1105928 | tf_op jit(solution)/shard_map/ppermute | solution.py:14
  17.1 21.9 %all-to-all-start = ((f32[8,16,896]{2,1,0:T(8,128)}), f32[8,16,896]{2,1,0:T(8,128)S(1)}, u32[]{:S(2)}, u32[]{:S(2)}) async-start(f32[8,16,896]{2,1,0:T(8,128)} %pad_maximum_fusion), calls=%async_computation | async-start | bytes 917504 | tf_op jit(solution)/shard_map/all_to_all | solution.py:62
  40.2 15.6 %all-to-all-start.1 = ((f32[8,16,768]{2,1,0:T(8,128)}), f32[8,16,768]{2,1,0:T(8,128)S(1)}, u32[]{:S(2)}, u32[]{:S(2)}) async-start(f32[8,16,768]{2,1,0:T(8,128)} %bitcast.6), calls=%async_computation.1 | async-start | bytes 786432 | tf_op jit(solution)/shard_map/all_to_all | solution.py:66
  56.9 0.8 copy-start.1
  62.6 90.1 %all-to-all-start.2 = ((f32[46,128,128]{2,0,1:T(8,128)}), f32[46,128,128]{2,0,1:T(8,128)S(1)}, u32[]{:S(2)}, u32[]{:S(2)}) async-start(f32[46,128,128]{2,0,1:T(8,128)} %copy.33), calls=%async_computation.2 | async-start | bytes 6291456 | tf_op jit(solution)/shard_map/all_to_all | solution.py:88
  154.0 1.4 copy-start.2

commit v9 on v8

--- a/solution.py
+++ b/solution.py
@@ -90,7 +90,9 @@
     slot_lanes = jnp.arange(slot_total, dtype=jnp.float32)[None, :]
     select_in = arrived[components] == slot_lanes
     filled = jnp.any(select_in, axis=0)
-    incoming = exact_select("is,qit->qst", select_in, arrived[:components])
+    incoming = jnp.einsum(
+        "is,qit->qst", select_in.astype(jnp.float32), arrived[:components], precision=highest
+    )
 
     old_t = store_old[0, 0].transpose(1, 0, 2).astype(jnp.float32)
     storage = jnp.where(filled[None, :, None], incoming, old_t).transpose(1, 0, 2)

time: 159 us -> 159 us (level)
    dot_general x6 -> x3, matrix products: 8.56 us -> 2.93 us  [exact_select(): jnp.einsum(spec, select, part.astype(jnp.bfloat16), preferred_element_typ...]
    dot_general x0 -> x1, matrix products: none -> 5.47 us  [local(): jnp.einsum('is,qit->qst', select_in.astype(jnp.float32), arrived[:compone...]
where the time goes in v9:
time: 159 us; the launch traced here: 158 us
  waiting for transfers between devices  97.6 us (61%)
  starting transfers between devices  40.3 us (25%)
  matrix products  10.1 us (6%)
  local copies, waits for them, and re-layouts  6.16 us (4%)
  other arithmetic  2.56 us (2%)
    all_to_all x1, waiting for transfers between devices, local(): arrived = lax.all_to_all(outgoing, 'blk', 1, 1, tiled=True)  71.4 us
    all_to_all x1, starting transfers between devices, local(): arrived = lax.all_to_all(outgoing, 'blk', 1, 1, tiled=True)  16.6 us
    all_to_all x1, waiting for transfers between devices, local(): lax.all_to_all(mixed.reshape(n_pitch, pitch_local, width), 'pitch', 0, 0,...  11.9 us
    all_to_all x1, waiting for transfers between devices, local(): gathered = lax.all_to_all(chunks, 'pitch', 0, 0, tiled=True)  10.8 us
    all_to_all x1, starting transfers between devices, local(): gathered = lax.all_to_all(chunks, 'pitch', 0, 0, tiled=True)  10 us
    ppermute x1, starting transfers between devices, with_halo(): high = lax.ppermute(block, axis, backward)  5.48 us
    dot_general x1, matrix products, local(): jnp.einsum('is,qit->qst', select_in.astype(jnp.float32), arrived[:compone...  5.47 us
    ppermute x1, starting transfers between devices, with_halo(): low = lax.ppermute(block, axis, forward)  4.71 us
  transfers between devices with their start and end apart: 5, of which 4 were waited for; matrix products, arithmetic and copies ran while one was open for 2% of the time, Pallas kernels for 0%

profile of v9, /device:TPU:1, one launch (start us, length us, event | category | flops | bytes accessed | tf_op | source)
XLA Modules:
  0.0 158.2 jit_solution(14286308378648832705)
XLA Ops:
  0.6 0.0 copy-start
  0.7 4.7 %collective-permute-start.1 = (f32[720,128]{1,0:T(8,128)}, f32[720,128]{1,0:T(8,128)S(1)}, u32[]{:S(2)}, u32[]{:S(2)}) collective-permute-start(f32[720,128]{1,0:T(8,128)} %bitcast.48), channel_id=1, source_target_pairs={{0,1},{1,2},{2,3},{3,4},{4,5},{5,6},{6,7},{7,8},{8,9},{9,10},{10,1... | collective-permute-start | bytes 1105928 | tf_op jit(solution)/shard_map/ppermute | solution.py:13
  5.4 5.5 %collective-permute-start = (f32[720,128]{1,0:T(8,128)}, f32[720,128]{1,0:T(8,128)S(1)}, u32[]{:S(2)}, u32[]{:S(2)}) collective-permute-start(f32[720,128]{1,0:T(8,128)} %bitcast.49), channel_id=1, source_target_pairs={{1,0},{2,1},{3,2},{4,3},{5,4},{6,5},{7,6},{8,7},{9,8},{10,9},{11,1... | collective-permute-start | bytes 1105928 | tf_op jit(solution)/shard_map/ppermute | solution.py:14
  10.9 3.5 %collective-permute-done = f32[720,128]{1,0:T(8,128)S(1)} collective-permute-done((f32[720,128]{1,0:T(8,128)}, f32[720,128]{1,0:T(8,128)S(1)}, u32[]{:S(2)}, u32[]{:S(2)}) %collective-permute-start) | collective-permute-done | bytes 368672 | tf_op jit(solution)/shard_map/ppermute | solution.py:14
  14.5 1.1 multiply_add_fusion
  15.6 0.5 fusion.9
  16.1 0.1 reshape.144
  16.1 0.1 copy.39
  16.3 0.8 pad_maximum_fusion
  17.1 10.0 %all-to-all-start = ((f32[8,16,896]{2,1,0:T(8,128)}), f32[8,16,896]{2,1,0:T(8,128)S(1)}, u32[]{:S(2)}, u32[]{:S(2)}) async-start(f32[8,16,896]{2,1,0:T(8,128)} %pad_maximum_fusion), calls=%async_computation | async-start | bytes 917504 | tf_op jit(solution)/shard_map/all_to_all | solution.py:62
  27.8 0.2 convert_reduce_fusion
  28.0 0.1 iota_compare_fusion.2
  28.1 0.1 iota_compare_fusion.1
  28.2 10.8 %all-to-all-done = f32[8,16,896]{2,1,0:T(8,128)S(1)} async-done(((f32[8,16,896]{2,1,0:T(8,128)}), f32[8,16,896]{2,1,0:T(8,128)S(1)}, u32[]{:S(2)}, u32[]{:S(2)}) %all-to-all-start) | async-done | bytes 458784 | tf_op jit(solution)/shard_map/all_to_all | solution.py:62
  39.0 1.2 fusion.7
  40.2 3.5 %all-to-all-start.1 = ((f32[8,16,768]{2,1,0:T(8,128)}), f32[8,16,768]{2,1,0:T(8,128)S(1)}, u32[]{:S(2)}, u32[]{:S(2)}) async-start(f32[8,16,768]{2,1,0:T(8,128)} %bitcast.6), calls=%async_computation.1 | async-start | bytes 786432 | tf_op jit(solution)/shard_map/all_to_all | solution.py:66
  43.7 0.1 select_reduce_fusion
  43.8 0.2 and_reduce_fusion
  44.0 11.9 %all-to-all-done.1 = f32[8,16,768]{2,1,0:T(8,128)S(1)} async-done(((f32[8,16,768]{2,1,0:T(8,128)}), f32[8,16,768]{2,1,0:T(8,128)S(1)}, u32[]{:S(2)}, u32[]{:S(2)}) %all-to-all-start.1) | async-done | bytes 393248 | tf_op jit(solution)/shard_map/all_to_all | solution.py:66
  55.9 0.1 reshape.147
  55.9 0.1 copy.26
  56.0 0.8 slice_bitcast_fusion
  56.9 0.6 fusion.13
  57.5 0.2 copy-done.1
  57.7 0.6 fusion.12
  58.3 1.7 %add_bitcast_fusion = f32[46,128,128]{1,2,0:T(8,128)S(1)} fusion(f32[46,128,128]{2,1,0:T(8,128)S(1)} %fusion.12, f32[46,128,128]{2,1,0:T(8,128)S(1)} %fusion.13, f32[46,17,128]{2,1,0:T(8,128)} %copy-done.1, bf16[128,1]{0,1:T(2,128)(2,1)S(1)} %convert_bitcast_fusion, bf16[128,16]{0,1:T(8,128)(2,1)S(1)} %convert_convert_fusion), kind=kOutput, calls=%fused_computation | convolution fusion | flops 27741184 | bytes 9448704 | tf_op jit(solution)/shard_map/sp,qpt->qst/dot_general | solution.py:26
  60.0 2.6 %copy.27 = f32[46,128,128]{2,0,1:T(8,128)} copy(f32[46,128,128]{1,2,0:T(8,128)S(1)} %add_bitcast_fusion) | data formatting | bytes 6029312 | tf_op jit(solution)/shard_map/add | solution.py:29
  62.6 16.6 %all-to-all-start.2 = ((f32[46,128,128]{2,0,1:T(8,128)}), f32[46,128,128]{2,0,1:T(8,128)S(1)}, u32[]{:S(2)}, u32[]{:S(2)}) async-start(f32[46,128,128]{2,0,1:T(8,128)} %copy.27), calls=%async_computation.2 | async-start | bytes 6291456 | tf_op jit(solution)/shard_map/all_to_all | solution.py:88
  79.2 2.1 %copy.30 = f32[16,1,45,128]{3,1,2,0:T(1,128)} copy(f32[16,1,45,128]{3,0,2,1:T(8,128)} %get-tuple-element.23) | data formatting | bytes 737280
  81.3 71.4 %all-to-all-done.2 = f32[46,128,128]{2,0,1:T(8,128)S(1)} async-done(((f32[46,128,128]{2,0,1:T(8,128)}), f32[46,128,128]{2,0,1:T(8,128)S(1)}, u32[]{:S(2)}, u32[]{:S(2)}) %all-to-all-start.2) | async-done | bytes 3014688 | tf_op jit(solution)/shard_map/all_to_all | solution.py:88
  152.7 0.1 slice.45
  152.8 5.5 %fusion.2 = f32[1,1,128,45,128]{4,2,3,1,0:T(8,128)} fusion(f32[45,128,128]{2,0,1:T(8,128)S(1)} %bitcast.43, bf16[1,1,128,45,128]{4,2,3,1,0:T(8,128)(2,1)} %param.13, pred[128]{0:T(512)(128)(4,1)S(1)} %get-tuple-element.20, pred[128,128]{1,0:T(32,128)(4,1)S(1)} %get-tuple-element.21), kind=kOutput, calls=%fused_computation.4 | convolution fusion | flops 1133936640 | bytes 7389312 | tf_op jit(solution)/shard_map/is,qit->qst/dot_general | solution.py:93
  (21 shorter events, 0.2 us)
Async XLA Ops:
  0.6 14.9 %copy-start = (f32[1,128,128]{2,1,0:T(8,128)S(1)}, f32[1,128,128]{2,1,0:T(8,128)}, u32[]{:S(2)}) copy-start(f32[1,128,128]{2,1,0:T(8,128)} %param.12) | copy-start | bytes 196612
  0.6 15.6 %copy-start.2 = (f32[1,16,128]{2,1,0:T(8,128)S(1)}, f32[1,16,128]{2,1,0:T(8,128)}, u32[]{:S(2)}) copy-start(f32[1,16,128]{2,1,0:T(8,128)} %param.11) | copy-start | bytes 24580
  0.7 26.5 %copy-start.5 = (s32[1,1,64]{2,1,0:T(1,128)S(1)}, s32[1,1,64]{2,1,0:T(1,128)}, u32[]{:S(2)}) copy-start(s32[1,1,64]{2,1,0:T(1,128)} %param.16) | copy-start | bytes 772
  0.7 27.1 %copy-start.4 = (s32[1,1,64]{2,1,0:T(1,128)S(1)}, s32[1,1,64]{2,1,0:T(1,128)}, u32[]{:S(2)}) copy-start(s32[1,1,64]{2,1,0:T(1,128)} %param.15) | copy-start | bytes 772
  0.7 27.4 %copy-start.3 = (s32[1,1,64]{2,1,0:T(1,128)S(1)}, s32[1,1,64]{2,1,0:T(1,128)}, u32[]{:S(2)}) copy-start(s32[1,1,64]{2,1,0:T(1,128)} %param.14) | copy-start | bytes 772
  0.7 10.2 %collective-permute-start.1 = (f32[720,128]{1,0:T(8,128)}, f32[720,128]{1,0:T(8,128)S(1)}, u32[]{:S(2)}, u32[]{:S(2)}) collective-permute-start(f32[720,128]{1,0:T(8,128)} %bitcast.48), channel_id=1, source_target_pairs={{0,1},{1,2},{2,3},{3,4},{4,5},{5,6},{6,7},{7,8},{8,9},{9,10},{10,1... | collective-permute-start | bytes 1105928 | tf_op jit(solution)/shard_map/ppermute | solution.py:13
  5.4 9.0 %collective-permute-start = (f32[720,128]{1,0:T(8,128)}, f32[720,128]{1,0:T(8,128)S(1)}, u32[]{:S(2)}, u32[]{:S(2)}) collective-permute-start(f32[720,128]{1,0:T(8,128)} %bitcast.49), channel_id=1, source_target_pairs={{1,0},{2,1},{3,2},{4,3},{5,4},{6,5},{7,6},{8,7},{9,8},{10,9},{11,1... | collective-permute-start | bytes 1105928 | tf_op jit(solution)/shard_map/ppermute | solution.py:14
  17.1 21.9 %all-to-all-start = ((f32[8,16,896]{2,1,0:T(8,128)}), f32[8,16,896]{2,1,0:T(8,128)S(1)}, u32[]{:S(2)}, u32[]{:S(2)}) async-start(f32[8,16,896]{2,1,0:T(8,128)} %pad_maximum_fusion), calls=%async_computation | async-start | bytes 917504 | tf_op jit(solution)/shard_map/all_to_all | solution.py:62
  40.2 15.6 %all-to-all-start.1 = ((f32[8,16,768]{2,1,0:T(8,128)}), f32[8,16,768]{2,1,0:T(8,128)S(1)}, u32[]{:S(2)}, u32[]{:S(2)}) async-start(f32[8,16,768]{2,1,0:T(8,128)} %bitcast.6), calls=%async_computation.1 | async-start | bytes 786432 | tf_op jit(solution)/shard_map/all_to_all | solution.py:66
  56.9 0.8 copy-start.1
  62.6 90.1 %all-to-all-start.2 = ((f32[46,128,128]{2,0,1:T(8,128)}), f32[46,128,128]{2,0,1:T(8,128)S(1)}, u32[]{:S(2)}, u32[]{:S(2)}) async-start(f32[46,128,128]{2,0,1:T(8,128)} %copy.27), calls=%async_computation.2 | async-start | bytes 6291456 | tf_op jit(solution)/shard_map/all_to_all | solution.py:88
